TPU v7x, 256 devices: a whole 4x4x8 slice. The times are simulated.
256 devices in a mesh: grp: 8 (over y, z_hi), tile: 32 (over z_lo, x, core).
Axes of the slice: x: 4, y: 4, z: 8 (z_hi: 2, z_lo: 4; z = z_hi * 4 + z_lo), core: 2. Of those that a mesh axis runs over, the one named last changes fastest.
Arguments:
- sensitivity: bfloat16 [16, 4096, 3, 1024], P('grp', 'tile'), may hold values from -6 to 6
- inst_weight: float32 [16], P('grp'), may hold values from 0.3 to 3
- filter_taps: bfloat16 [129], replicated, may hold values from 0.019897461 to 0.13964844
- basis_rows: bfloat16 [128, 16], replicated, may hold values from -0.5 to 0.5
- basis_cols: bfloat16 [128, 16], replicated, may hold values from -0.5 to 0.5
- box_table: int32 [256, 1], replicated, may hold values from 0 to 255
- owner_perm: int32 [256], replicated, may hold values from 0 to 255, each once
Outputs:
- design_grad: float32 [256, 3, 256], P(('grp', 'tile'))
Inputs may be any that keep to these rules, and one draw needn't show every extreme that they name: `box_table`: every one of the 256 boxes is named by at least one tile. `owner_perm`: each box appears exactly once.
All inputs are finite; a program needn't handle non-finite values.
Results may differ from a plain program's by a relative error of at most 0.017.
Values may be sent and summed in bfloat16 or wider, within the bound.
No kernel may reach another device: no remote copies, remote signals or barrier semaphores. Data moves between devices by JAX's collectives and lax.ppermute only.
A program may use at most 64 MiB of HBM per device.

v0:
```python
import jax
import jax.numpy as jnp
from jax import lax
from jax.sharding import PartitionSpec as P


def band_matrix(filter_taps, inputs, outputs):
    reach = filter_taps.shape[0] - 1
    period = jnp.concatenate([filter_taps, jnp.zeros((inputs - reach,), filter_taps.dtype)])
    repeated = jnp.broadcast_to(period[None, :], (outputs, inputs + 1)).reshape(-1)
    return repeated[: outputs * inputs].reshape(outputs, inputs).T


def smooth_columns(field, filter_taps):
    reach = filter_taps.shape[0] - 1
    half = reach // 2
    width = field.shape[2]
    block = min(1024, width)
    padded = jnp.pad(field, ((0, 0), (0, 0), (half, half)))
    flat = padded.reshape(-1, width + reach)
    matrix = band_matrix(filter_taps, block + reach, block)
    pieces = jnp.dot(flat, matrix, preferred_element_type=jnp.float32)
    return pieces.reshape(field.shape).astype(jnp.bfloat16)


def smooth_rows_whole(field, filter_taps):
    reach = filter_taps.shape[0] - 1
    half = reach // 2
    height = field.shape[0]
    block = min(1024, height)
    padded = jnp.pad(field, ((half, half), (0, 0), (0, 0)))
    flat = padded.reshape(height + reach, -1)
    matrix = band_matrix(filter_taps, block + reach, block).T
    starts = jnp.arange(height // block, dtype=jnp.int32) * block

    def one_block(start):
        window = lax.dynamic_slice_in_dim(flat, start, block + reach, 0)
        return jnp.dot(matrix, window, preferred_element_type=jnp.float32)

    result = lax.map(one_block, starts)
    return result.reshape(field.shape).astype(jnp.bfloat16)


def contract_tiles(second, row_start, col_start, cols_all, basis_rows, basis_cols, box_table):
    local_rows = second.shape[0]
    local_cols = second.shape[2]
    tile_rows = basis_rows.shape[0]
    tile_cols = basis_cols.shape[0]
    ctrl_rows = basis_rows.shape[1]
    ctrl_cols = basis_cols.shape[1]
    row_tiles = local_rows // tile_rows
    shaped = second.reshape(row_tiles, tile_rows, 3, local_cols)
    rowwise = jnp.einsum("takc,ap->tkpc", shaped, basis_rows, preferred_element_type=jnp.float32)
    columns = col_start + jnp.arange(local_cols, dtype=jnp.int32)
    local_basis = basis_cols[columns % tile_cols].astype(jnp.float32)
    col_tiles = 1
    which_tile = jnp.zeros((local_cols,), jnp.int32)
    select = (which_tile[:, None] == jnp.arange(col_tiles, dtype=jnp.int32)[None, :]).astype(
        jnp.float32
    )
    spread = (local_basis[:, None, :] * select[:, :, None]).reshape(
        local_cols, col_tiles * ctrl_cols
    )
    tile_part = jnp.einsum("tkpc,cm->tkpm", rowwise, spread, precision=lax.Precision.HIGHEST)
    tile_part = tile_part.reshape(row_tiles, 3, ctrl_rows, col_tiles, ctrl_cols)
    tile_part = tile_part.transpose(0, 3, 1, 2, 4).reshape(
        row_tiles * col_tiles, 3 * ctrl_rows * ctrl_cols
    )
    tile_row_ids = row_start // tile_rows + jnp.arange(row_tiles, dtype=jnp.int32)
    tile_col_ids = col_start // tile_cols + jnp.arange(col_tiles, dtype=jnp.int32)
    tile_ids = (tile_row_ids[:, None] * (cols_all // tile_cols) + tile_col_ids[None, :]).reshape(-1)
    tile_boxes = box_table[tile_ids, 0]
    return (tile_part, tile_boxes)


def to_slots(tile_part, tile_boxes, slot_boxes):
    onehot = (tile_boxes[:, None] == slot_boxes[None, :]).astype(jnp.float32)
    return jnp.dot(onehot.T, tile_part, precision=lax.Precision.HIGHEST)


def local(sensitivity, inst_weight, filter_taps, basis_rows, basis_cols, box_table, owner_perm):
    cols_all = sensitivity.shape[3]
    ctrl_count = basis_rows.shape[1] * basis_cols.shape[1]
    summed = jnp.sum(
        sensitivity.astype(jnp.float32) * inst_weight[:, None, None, None], axis=0
    ).astype(jnp.bfloat16)
    first = smooth_columns(summed, filter_taps)
    strips = lax.all_to_all(first, "tile", split_axis=2, concat_axis=0, tiled=True)
    second = smooth_rows_whole(strips, filter_taps)
    col_start = lax.axis_index("tile") * strips.shape[2]
    tile_part, tile_boxes = contract_tiles(
        second, 0, col_start, cols_all, basis_rows, basis_cols, box_table
    )
    ordered = to_slots(tile_part, tile_boxes, owner_perm)
    owned = lax.psum_scatter(ordered, ("grp", "tile"), scatter_dimension=0, tiled=True)
    return owned.reshape(-1, 3, ctrl_count)


def solution(mesh):
    placed = (P("grp", "tile", None, None), P("grp"), P(), P(), P(), P(), P())
    return jax.shard_map(
        local, mesh=mesh, in_specs=placed, out_specs=P(("grp", "tile"), None, None), check_vma=False
    )
```

profile of v0, /device:TPU:1, one launch (start us, length us, event | category | flops | bytes accessed | tf_op | source)
XLA Modules:
  0.0 342.2 jit_solution(4403532589106235172)
XLA Ops:
  6.5 0.0 copy-start
  6.5 0.7 concatenate.8
  7.2 0.2 broadcast_in_dim.8
  7.4 5.3 %reshape.101 = bf16[1180672]{0:T(1024)(128)(2,1)} reshape(bf16[1024,1153]{1,0:T(8,128)(2,1)S(1)} %broadcast_in_dim.8) | data formatting | bytes 4722688 | tf_op jit(solution)/shard_map/reshape | solution.py:10
  12.7 1.7 slice.9
  14.4 0.0 copy-start.2
  14.4 0.0 copy-start.6
  14.4 3.8 %reshape.119 = bf16[1024,1152,1]{1,0,2:T(8,128)(2,1)} reshape(bf16[1179648]{0:T(1024)(128)(2,1)S(1)} %slice.9) | data formatting | bytes 4718592 | tf_op jit(solution)/shard_map/reshape | solution.py:11
  18.2 0.0 copy-done.6
  18.2 2.0 multiply_reduce_fusion
  20.2 0.0 copy-done.2
  20.2 0.1 copy-done.3
  20.4 1.2 convolution_convert_fusion
  21.6 1.4 copy.18
  23.0 10.0 %all-to-all-start = ((bf16[128,3,1024]{0,1,2:T(4,128)(2,1)}), bf16[128,3,1024]{0,1,2:T(4,128)(2,1)S(1)}, u32[]{:S(2)}, u32[]{:S(2)}) async-start(bf16[128,3,1024]{0,1,2:T(4,128)(2,1)} %copy.18), calls=%async_computation | async-start | bytes 2097152 | tf_op jit(solution)/shard_map/all_to_all | solution.py:88
  33.1 0.0 all-reduce.7.cloned.1.call-start
  33.1 0.0 copy-start.4
  33.1 0.0 copy-start.1
  33.2 4.6 %reshape.102 = bf16[1024,1152]{1,0:T(8,128)(2,1)S(1)} reshape(bf16[1179648]{0:T(1024)(128)(2,1)} %copy-done.2) | data formatting | bytes 4718592 | tf_op jit(solution)/shard_map/reshape | solution.py:11
  37.8 0.0 copy-done.4
  37.8 0.1 copy.23
  38.0 0.0 copy-done.1
  38.0 0.7 gather_fusion
  38.7 0.6 gather_fusion.1
  39.3 20.4 %all-to-all-done = bf16[128,3,1024]{0,1,2:T(4,128)(2,1)S(1)} async-done(((bf16[128,3,1024]{0,1,2:T(4,128)(2,1)}), bf16[128,3,1024]{0,1,2:T(4,128)(2,1)S(1)}, u32[]{:S(2)}, u32[]{:S(2)}) %all-to-all-start) | async-done | bytes 786464 | tf_op jit(solution)/shard_map/all_to_all | solution.py:88
  59.7 0.1 copy.19
  59.8 0.2 copy.35
  60.0 0.3 pad.11
  60.3 15.9 %while.10 = (s32[]{:T(128)}, bf16[4,1024,96]{1,2,0:T(8,128)(2,1)}, s32[4]{0:T(128)S(1)}, bf16[4224,96]{0,1:T(8,128)(2,1)S(1)}, bf16[1024,1152]{1,0:T(8,128)(2,1)S(1)}, /*index=5*/s32[]{:T(128)}, s32[]{:T(128)}, s32[]{:T(128)}) while((s32[]{:T(128)}, bf16[4,1024,96]{1,2,0:T(8,128)(2,1)}, s32[4]{0:T(128)S(1)}, bf16[4224,96]{0,1:T(8,128)(2,1)S(1)}, ...), condition=%wide.region_2.3_spmd, body=%wide.region_1.2_spmd.sunk | while | flops 226492416 | bytes 2974343 | solution.py:40
  60.3 0.6 dynamic_slice.12
  62.7 1.5 fusion.26
  64.2 0.6 dynamic_slice.12
  66.7 1.5 fusion.26
  68.2 0.6 dynamic_slice.12
  70.6 1.5 fusion.26
  72.2 0.6 dynamic_slice.12
  74.6 1.5 fusion.26
  76.2 1.7 copy.22
  77.9 0.0 copy-start.5
  77.9 0.3 convert_element_type.26
  78.2 0.0 copy-done
  78.2 1.1 convolution_bitcast_fusion.1
  79.4 0.6 fusion.4
  80.0 0.0 copy-done.5
  80.0 1.5 fusion.6
  81.5 0.0 all-reduce.7.cloned.1.call-update
  81.5 252.5 %all-reduce.7.cloned.1.call-done = f32[256,768]{1,0:T(8,128)} async-done(((f32[256,768]{1,0:T(8,128)}), f32[256,768]{1,0:T(8,128)}) %all-reduce.7.cloned.1.call-update) | async-done | bytes 786448
  334.0 1.3 constant_dynamic-slice_fusion
  (6 shorter events, 0.0 us)
Async XLA Ops:
  6.5 71.7 %copy-start = (bf16[128,16]{0,1:T(8,128)(2,1)S(1)}, bf16[128,16]{0,1:T(8,128)(2,1)}, u32[]{:S(2)}) copy-start(bf16[128,16]{0,1:T(8,128)(2,1)} %param.12) | copy-start | bytes 12292
  14.4 5.8 %copy-start.2 = (bf16[1179648]{0:T(1024)(128)(2,1)}, bf16[1179648]{0:T(1024)(128)(2,1)S(1)}, u32[]{:S(2)}) copy-start(bf16[1179648]{0:T(1024)(128)(2,1)S(1)} %slice.9) | copy-start | bytes 7077892
  14.4 3.8 %copy-start.6 = (f32[2]{0:T(128)S(1)}, f32[2]{0:T(128)}, u32[]{:S(2)}) copy-start(f32[2]{0:T(128)} %param.10) | copy-start | bytes 28
  18.2 2.1 copy-start.3
  23.0 36.6 %all-to-all-start = ((bf16[128,3,1024]{0,1,2:T(4,128)(2,1)}), bf16[128,3,1024]{0,1,2:T(4,128)(2,1)S(1)}, u32[]{:S(2)}, u32[]{:S(2)}) async-start(bf16[128,3,1024]{0,1,2:T(4,128)(2,1)} %copy.18), calls=%async_computation | async-start | bytes 2097152 | tf_op jit(solution)/shard_map/all_to_all | solution.py:88
  33.1 300.9 %all-reduce.7.cloned.1.call-start = ((), (), s32[]{:S(2)}) async-start(), calls=%async_computation.1 | async-start | bytes 1572864
  33.1 4.7 %copy-start.4 = (bf16[128,16]{0,1:T(8,128)(2,1)S(1)}, bf16[128,16]{0,1:T(8,128)(2,1)}, u32[]{:S(2)}) copy-start(bf16[128,16]{0,1:T(8,128)(2,1)} %param.13) | copy-start | bytes 12292
  33.1 4.8 %copy-start.1 = (s32[256,1]{0,1:T(1,128)S(1)}, s32[256,1]{0,1:T(1,128)}, u32[]{:S(2)}) copy-start(s32[256,1]{0,1:T(1,128)} %param.14) | copy-start | bytes 3076
  77.9 2.1 copy-start.5
Sparse Core Ops, SparseCore 0:
  81.6 252.3 all-reduce.6
where the time goes:
time: 343 us; the launch traced here: 342 us
  waiting for transfers between devices  273 us (80%)
  local copies, waits for them, and re-layouts  25.7 us (7%)
  between operations  13.6 us (4%)
  matrix products  10.6 us (3%)
  starting transfers between devices  10.1 us (3%)
  loops' own time  7.29 us (2%)
    unnamed x2, waiting for transfers between devices  253 us
    all_to_all x1, waiting for transfers between devices, local(): lax.all_to_all(first, 'tile', split_axis=2, concat_axis=0, tiled=True)  20.4 us
    all_to_all x1, starting transfers between devices, local(): lax.all_to_all(first, 'tile', split_axis=2, concat_axis=0, tiled=True)  10 us
    reshape x2, local copies, waits for them, and re-layouts, band_matrix(): return repeated[:outputs * inputs].reshape(outputs, inputs).T  8.42 us
    another operation x1, loops' own time, smooth_rows_whole(): result = lax.map(one_block, starts)  7.29 us
  transfers between devices with their start and end apart: 2, of which 2 were waited for; matrix products, arithmetic and copies ran while one was open for 2% of the time, Pallas kernels for 0%

commit v1 on v0

v1 whole, which is shorter than its diff:
```python
import jax
import jax.numpy as jnp
from jax import lax
from jax.sharding import PartitionSpec as P


def smoothed_basis(filter_taps, basis):
    reach = filter_taps.shape[0] - 1
    length = basis.shape[0]
    span = length + 2 * (reach // 2)
    offs = jnp.arange(span, dtype=jnp.int32)[:, None] - jnp.arange(length, dtype=jnp.int32)[None, :]
    taps = filter_taps.astype(jnp.float32)
    band = jnp.where((offs >= 0) & (offs <= reach), taps[jnp.clip(offs, 0, reach)], 0.0)
    return jnp.dot(band, basis.astype(jnp.float32), precision=lax.Precision.HIGHEST)


def window_blocks(extended, length):
    half = (extended.shape[0] - length) // 2
    padded = jnp.pad(extended, ((length - half, length - half), (0, 0)))
    return padded.reshape(3, length, -1)


def local(sensitivity, inst_weight, filter_taps, basis_rows, basis_cols, box_table, owner_perm):
    tile_rows, ctrl_rows = basis_rows.shape
    tile_cols, ctrl_cols = basis_cols.shape
    local_rows = sensitivity.shape[1]
    cols_all = sensitivity.shape[3]
    col_tiles = cols_all // tile_cols
    comps = sensitivity.shape[2]
    slots = owner_perm.shape[0]

    summed = jnp.sum(
        sensitivity.astype(jnp.float32) * inst_weight[:, None, None, None], axis=0
    ).astype(jnp.bfloat16)

    col_blocks = window_blocks(smoothed_basis(filter_taps, basis_cols), tile_cols)
    col_shift = (
        jnp.arange(col_tiles, dtype=jnp.int32)[:, None]
        - jnp.arange(col_tiles, dtype=jnp.int32)[None, :]
        + 1
    )
    col_valid = (col_shift >= 0) & (col_shift <= 2)
    col_matrix = jnp.where(
        col_valid[:, None, :, None],
        col_blocks[jnp.clip(col_shift, 0, 2)].transpose(0, 2, 1, 3),
        0.0,
    ).reshape(cols_all, col_tiles * ctrl_cols)
    col_hi = col_matrix.astype(jnp.bfloat16)
    col_lo = (col_matrix - col_hi.astype(jnp.float32)).astype(jnp.bfloat16)
    flat = summed.reshape(local_rows * comps, cols_all)
    by_cols = jnp.dot(flat, col_hi, preferred_element_type=jnp.float32) + jnp.dot(
        flat, col_lo, preferred_element_type=jnp.float32
    )
    by_cols = by_cols.reshape(local_rows, comps * col_tiles * ctrl_cols)

    assert local_rows == tile_rows
    row_blocks = window_blocks(smoothed_basis(filter_taps, basis_rows), tile_rows)[::-1]
    row_matrix = row_blocks.transpose(0, 2, 1).reshape(3 * ctrl_rows, local_rows)
    parts = jnp.dot(row_matrix, by_cols, precision=lax.Precision.HIGHEST)
    parts = parts.reshape(3, ctrl_rows, comps, col_tiles, ctrl_cols)
    parts = parts.transpose(0, 3, 2, 1, 4).reshape(3 * col_tiles, comps * ctrl_rows * ctrl_cols)

    tile_of_box = jnp.zeros((slots,), jnp.int32).at[box_table[:, 0]].set(
        jnp.arange(slots, dtype=jnp.int32)
    )
    tile_of_slot = tile_of_box[owner_perm]
    here = lax.axis_index("tile")
    rel_row = tile_of_slot // col_tiles - here + 1
    pick = rel_row * col_tiles + tile_of_slot % col_tiles
    mine = (rel_row >= 0) & (rel_row <= 2)
    outgoing = jnp.where(mine[:, None], parts[jnp.clip(pick, 0, 3 * col_tiles - 1)], 0.0)
    incoming = lax.all_to_all(outgoing, ("grp", "tile"), 0, 0, tiled=True)
    return jnp.sum(incoming, axis=0).reshape(1, comps, ctrl_rows * ctrl_cols)


def solution(mesh):
    placed = (P("grp", "tile", None, None), P("grp"), P(), P(), P(), P(), P())
    return jax.shard_map(
        local, mesh=mesh, in_specs=placed, out_specs=P(("grp", "tile"), None, None), check_vma=False
    )
```

time: 343 us -> 259 us (0.76)
  waiting for transfers between devices: 273 us -> 0 us
  local copies, waits for them, and re-layouts: 25.7 us -> 212 us
  blocking collectives: 0 us -> 41 us
  between operations: 13.6 us -> 0.29 us
  starting transfers between devices: 10.1 us -> 0 us
  matrix products: 10.6 us -> 2.92 us
  loops' own time: 7.29 us -> 0 us
    unnamed x2 -> x0, waiting for transfers between devices: 253 us -> none
    gather x2 -> x4, local copies, waits for them, and re-layouts: 1.29 us -> 206 us  [the longest x1 202 us: smoothed_basis(): taps[jnp.clip(offs, 0, reach)]]
    all_to_all x0 -> x1, blocking collectives: none -> 41 us  [local(): incoming = lax.all_to_all(outgoing, ('grp', 'tile'), 0, 0, tiled=True)]
    all_to_all x1 -> x0, waiting for transfers between devices: 20.4 us -> none  [local(): lax.all_to_all(first, 'tile', split_axis=2, concat_axis=0, tiled=True)]
    reshape x3 -> x5, local copies, waits for them, and re-layouts: 13.7 us -> 1.01 us  [the longest x1 0.59 us: local(): return jnp.sum(incoming, axis=0).reshape(1, comps, ctrl_rows * ctrl_cols)]
    all_to_all x1 -> x0, starting transfers between devices: 10 us -> none  [local(): lax.all_to_all(first, 'tile', split_axis=2, concat_axis=0, tiled=True)]
    dot_general x8 -> x5, matrix products: 10.6 us -> 2.92 us  [the longest x1 1.8 us: local(): parts = jnp.dot(row_matrix, by_cols, precision=lax.Precision.HIGHEST)]
    another operation x1 -> x0, loops' own time: 7.29 us -> none  [smooth_rows_whole(): result = lax.map(one_block, starts)]
  transfers between devices with their start and end apart: 2 -> 0, of which waited for: 2 -> 0; matrix products, arithmetic and copies ran while one was open for 2% -> 0% of each run, Pallas kernels for 0% -> 0%
where the time goes in v1:
time: 259 us; the launch traced here: 258 us
  local copies, waits for them, and re-layouts  212 us (82%)
  blocking collectives  41 us (16%)
  matrix products  2.92 us (1%)
    gather x1, local copies, waits for them, and re-layouts, smoothed_basis(): taps[jnp.clip(offs, 0, reach)]  202 us
    all_to_all x1, blocking collectives, local(): incoming = lax.all_to_all(outgoing, ('grp', 'tile'), 0, 0, tiled=True)  41 us

profile of v1, /device:TPU:1, one launch (start us, length us, event | category | flops | bytes accessed | tf_op | source)
XLA Modules:
  0.0 258.3 jit_solution(9709434356209648512)
XLA Ops:
  0.0 0.0 copy-start
  0.0 0.1 fusion.7
  0.1 0.7 convert_element_type.46
  0.8 202.2 %gather_fusion.1 = f32[32768]{0:T(1024)S(1)} fusion(f32[129]{0:T(256)S(1)} %convert_element_type.46, s32[32768]{0:T(1024)S(1)} %fusion.7), kind=kCustom, calls=%fused_computation.1 | custom fusion | bytes 393216 | tf_op jit(solution)/shard_map/gather | solution.py:13
  203.0 0.0 copy-done
  203.0 0.2 fusion.11
  203.2 0.1 copy_bitcast_fusion
  203.3 0.1 reshape.259
  203.4 0.6 gather_fusion.2
  204.0 0.0 copy-start.1
  204.0 0.0 copy-start.4
  204.0 0.3 bitcast_convert_fusion
  204.4 0.3 fusion
  204.7 0.7 copy-done.1
  205.4 0.0 copy-done.4
  205.4 0.4 multiply_reduce_fusion
  205.9 0.7 copy.15
  206.6 0.7 convert_element_type.49
  207.3 0.0 copy-start.5
  207.3 0.4 fusion.3
  207.6 0.4 convolution_add_fusion
  208.1 0.1 copy.18
  208.2 0.0 copy-done.5
  208.2 0.0 copy-start.2
  208.2 0.0 copy-start.3
  208.2 0.2 fusion.12
  208.4 0.1 pad.7
  208.6 1.8 convolution_bitcast_fusion
  210.5 0.3 reshape.239
  210.7 0.0 copy-done.2
  210.7 0.0 copy-done.3
  210.8 1.4 scatter_custom_fusion
  212.2 1.9 gather_fusion
  214.2 1.1 gather_fusion.3
  215.3 0.1 bitcast_select_fusion
  215.4 0.8 copy.21
  216.2 41.0 %all_to_all.6 = f32[256,1,768]{2,1,0:T(1,128)S(1)} all-to-all(f32[256,1,768]{2,1,0:T(1,128)S(1)} %copy.21), channel_id=1, replica_groups=mesh['grp'=8,'tile'=32] {'grp','tile'}, dimensions={0} | all-to-all | bytes 1572864 | tf_op jit(solution)/shard_map/all_to_all | solution.py:72
  257.2 0.5 reduce_sum.19
  257.8 0.6 reshape.240
  (14 shorter events, 0.2 us)
Async XLA Ops:
  0.0 203.0 %copy-start = (bf16[128,16]{0,1:T(8,128)(2,1)S(1)}, bf16[128,16]{0,1:T(8,128)(2,1)}, u32[]{:S(2)}) copy-start(bf16[128,16]{0,1:T(8,128)(2,1)} %param.11) | copy-start | bytes 12292
  204.0 1.4 copy-start.1
  204.0 1.4 copy-start.4
  207.3 0.9 copy-start.5
  208.2 2.5 copy-start.2
  208.2 2.5 copy-start.3

commit v2 on v1

--- a/solution.py
+++ b/solution.py
@@ -6,12 +6,12 @@
 
 def smoothed_basis(filter_taps, basis):
     reach = filter_taps.shape[0] - 1
-    length = basis.shape[0]
-    span = length + 2 * (reach // 2)
-    offs = jnp.arange(span, dtype=jnp.int32)[:, None] - jnp.arange(length, dtype=jnp.int32)[None, :]
-    taps = filter_taps.astype(jnp.float32)
-    band = jnp.where((offs >= 0) & (offs <= reach), taps[jnp.clip(offs, 0, reach)], 0.0)
-    return jnp.dot(band, basis.astype(jnp.float32), precision=lax.Precision.HIGHEST)
+    lines = basis.astype(jnp.float32).T[:, None, :]
+    kernel = filter_taps.astype(jnp.float32)[::-1][None, None, :]
+    full = lax.conv_general_dilated(
+        lines, kernel, (1,), [(reach, reach)], precision=lax.Precision.HIGHEST
+    )
+    return full[:, 0, :].T
 
 
 def window_blocks(extended, length):
@@ -60,10 +60,10 @@
     parts = parts.reshape(3, ctrl_rows, comps, col_tiles, ctrl_cols)
     parts = parts.transpose(0, 3, 2, 1, 4).reshape(3 * col_tiles, comps * ctrl_rows * ctrl_cols)
 
-    tile_of_box = jnp.zeros((slots,), jnp.int32).at[box_table[:, 0]].set(
-        jnp.arange(slots, dtype=jnp.int32)
+    tiles = jnp.arange(box_table.shape[0], dtype=jnp.int32)
+    tile_of_slot = jnp.sum(
+        jnp.where(box_table[:, 0][None, :] == owner_perm[:, None], tiles[None, :], 0), axis=1
     )
-    tile_of_slot = tile_of_box[owner_perm]
     here = lax.axis_index("tile")
     rel_row = tile_of_slot // col_tiles - here + 1
     pick = rel_row * col_tiles + tile_of_slot % col_tiles

time: 259 us -> 59 us (0.23)
  local copies, waits for them, and re-layouts: 212 us -> 8.5 us
  matrix products: 2.92 us -> 7.5 us
    gather x2 -> x0, local copies, waits for them, and re-layouts: 204 us -> none  [the longest x1 202 us: smoothed_basis(): taps[jnp.clip(offs, 0, reach)]]
    conv_general_dilated x0 -> x2, matrix products: none -> 4.93 us  [smoothed_basis(): lax.conv_general_dilated(lines, kernel, (1,), [(reach, reach)], precision...]
where the time goes in v2:
time: 59 us; the launch traced here: 58.9 us
  blocking collectives  41 us (69%)
  local copies, waits for them, and re-layouts  8.5 us (14%)
  matrix products  7.5 us (13%)
  other arithmetic  1.62 us (3%)
    all_to_all x1, blocking collectives, local(): incoming = lax.all_to_all(outgoing, ('grp', 'tile'), 0, 0, tiled=True)  41 us
    conv_general_dilated x2, matrix products, smoothed_basis(): lax.conv_general_dilated(lines, kernel, (1,), [(reach, reach)], precision...  4.93 us
    dot_general x1, matrix products, local(): parts = jnp.dot(row_matrix, by_cols, precision=lax.Precision.HIGHEST)  1.82 us
    convert_element_type x2, local copies, waits for them, and re-layouts, local(): summed = jnp.sum(sensitivity.astype(jnp.float32) * inst_weight[:, None, N...  1.37 us

profile of v2, /device:TPU:1, one launch (start us, length us, event | category | flops | bytes accessed | tf_op | source)
XLA Modules:
  0.0 58.9 jit_solution(16370256941117277514)
XLA Ops:
  0.0 0.9 %reshape.240 = bf16[1,1,129]{1,0,2:T(2,128)(2,1)S(1)} reshape(bf16[129]{0:T(256)(128)(2,1)} %param.9) | data formatting | bytes 516 | tf_op jit(solution)/shard_map/reshape.202
  0.9 0.8 %copy.55 = bf16[16,1,128]{0,1,2:T(2,128)(2,1)S(1)} copy(bf16[16,1,128]{2,0,1:T(8,128)(2,1)} %bitcast.76) | data formatting | bytes 8192 | tf_op jit(solution)/shard_map/broadcast_in_dim | solution.py:9
  1.7 2.5 %fusion.12 = f32[16,1,256]{0,1,2:T(1,128)S(1)} fusion(bf16[1,1,129]{1,0,2:T(2,128)(2,1)S(1)} %reshape.240, bf16[16,1,128]{0,1,2:T(2,128)(2,1)S(1)} %copy.55), kind=kOutput, calls=%fused_computation.36 | convolution fusion | flops 528384 | bytes 20738 | tf_op jit(solution)/shard_map/conv_general_dilated | solution.py:11
  4.2 0.1 copy.56
  4.3 0.1 reshape.223
  4.4 0.6 %gather_fusion = f32[64,128,16]{1,2,0:T(8,128)S(1)} fusion(f32[3,128,16]{1,2,0:T(8,128)S(1)} %copy.56, s32[1024]{0:T(1024)S(1)} %pad_clamp_fusion.1), kind=kCustom, calls=%fused_computation | custom fusion | bytes 1048832 | tf_op jit(solution)/shard_map/gather | solution.py:45
  5.0 0.0 copy-start
  5.0 0.0 copy-start.4
  5.0 0.1 bitcast_convert_fusion
  5.2 0.1 fusion
  5.3 1.1 %copy-done = bf16[2,128,3,1024]{3,1,2,0:T(8,128)(2,1)S(1)} copy-done((bf16[2,128,3,1024]{3,1,2,0:T(8,128)(2,1)S(1)}, bf16[2,128,3,1024]{3,1,2,0:T(8,128)(2,1)}, u32[]{:S(2)}) %copy-start) | copy-done | bytes 1572888
  6.4 0.0 copy-done.4
  6.4 0.4 multiply_reduce_fusion
  6.9 0.7 %copy.53 = bf16[128,3,1024]{2,1,0:T(4,128)(2,1)S(1)} copy(bf16[128,3,1024]{2,0,1:T(8,128)(2,1)S(1)} %multiply_reduce_fusion) | data formatting | bytes 1572864 | tf_op jit(solution)/shard_map/convert_element_type | solution.py:34
  7.6 0.7 %convert_element_type.46 = bf16[384,1024]{1,0:T(8,128)(2,1)S(1)} reshape(bf16[128,3,1024]{2,1,0:T(4,128)(2,1)S(1)} %copy.53) | data formatting | bytes 1572864 | tf_op jit(solution)/shard_map/convert_element_type | solution.py:34
  8.3 0.2 copy.57
  8.4 0.2 copy.58
  8.6 0.0 copy-start.1
  8.6 0.4 fusion.3
  9.0 0.4 convolution_add_fusion
  9.4 0.1 copy.59
  9.6 0.0 copy-done.1
  9.6 0.1 copy.51
  9.7 2.5 %fusion.11 = f32[16,1,256]{0,1,2:T(1,128)S(1)} fusion(bf16[1,1,129]{1,0,2:T(2,128)(2,1)S(1)} %reshape.240, bf16[16,1,128]{0,1,2:T(2,128)(2,1)S(1)} %copy.51), kind=kOutput, calls=%fused_computation.35 | convolution fusion | flops 528384 | bytes 20738 | tf_op jit(solution)/shard_map/conv_general_dilated | solution.py:11
  12.2 0.0 copy-start.2
  12.2 0.0 copy-start.3
  12.2 0.1 copy.52
  12.3 1.8 %convolution_bitcast_fusion = f32[3,8,3,16,16]{4,3,1,2,0:T(8,128)S(1)} fusion(f32[3,8,16,128,1]{3,2,1,0,4:T(8,128)S(1)} %bitcast.72, f32[3,128,16]{1,2,0:T(8,128)S(1)} %rev.2), kind=kOutput, calls=%fused_computation.3 | convolution fusion | flops 28311552 | bytes 294912 | tf_op jit(solution)/shard_map/dot_general | solution.py:59
  14.2 0.3 reshape.219
  14.4 0.0 copy-done.2
  14.4 0.0 copy-done.3
  14.4 0.2 select_reduce_fusion
  14.7 1.1 %gather_fusion.1 = f32[256,768]{1,0:T(8,128)S(1)} fusion(f32[24,768]{1,0:T(8,128)S(1)} %reshape.219, s32[1024]{0:T(1024)S(1)} %pad_clamp_fusion), kind=kCustom, calls=%fused_computation.1 | custom fusion | bytes 1573888 | tf_op jit(solution)/shard_map/gather | solution.py:71
  15.8 0.1 bitcast_select_fusion
  15.9 0.8 %copy.61 = f32[256,1,768]{2,1,0:T(1,128)S(1)} copy(f32[256,1,768]{2,0,1:T(8,128)S(1)} %bitcast_select_fusion) | data formatting | bytes 1572864 | tf_op jit(solution)/shard_map/jit(_where)/select_n | solution.py:71
  16.7 41.0 %all_to_all.6 = f32[256,1,768]{2,1,0:T(1,128)S(1)} all-to-all(f32[256,1,768]{2,1,0:T(1,128)S(1)} %copy.61), channel_id=1, replica_groups=mesh['grp'=8,'tile'=32] {'grp','tile'}, dimensions={0} | all-to-all | bytes 1572864 | tf_op jit(solution)/shard_map/all_to_all | solution.py:72
  57.7 0.5 reduce_sum.32
  58.3 0.6 %reshape.220 = f32[1,3,256]{2,0,1:T(1,128)} reshape(f32[768]{0:T(1024)S(1)} %reduce_sum.32) | data formatting | bytes 6144 | tf_op jit(solution)/shard_map/reshape | solution.py:73
  (11 shorter events, 0.2 us)
Async XLA Ops:
  5.0 1.4 %copy-start = (bf16[2,128,3,1024]{3,1,2,0:T(8,128)(2,1)S(1)}, bf16[2,128,3,1024]{3,1,2,0:T(8,128)(2,1)}, u32[]{:S(2)}) copy-start(bf16[2,128,3,1024]{3,1,2,0:T(8,128)(2,1)} %param.7) | copy-start | bytes 4718596
  5.0 1.4 %copy-start.4 = (f32[2]{0:T(128)S(1)}, f32[2]{0:T(128)}, u32[]{:S(2)}) copy-start(f32[2]{0:T(128)} %param.8) | copy-start | bytes 28
  8.6 1.0 %copy-start.1 = (bf16[128,16]{0,1:T(8,128)(2,1)S(1)}, bf16[128,16]{0,1:T(8,128)(2,1)}, u32[]{:S(2)}) copy-start(bf16[128,16]{0,1:T(8,128)(2,1)} %param.10) | copy-start | bytes 12292
  12.2 2.3 %copy-start.2 = (s32[256,1]{0,1:T(1,128)S(1)}, s32[256,1]{0,1:T(1,128)}, u32[]{:S(2)}) copy-start(s32[256,1]{0,1:T(1,128)} %param.12) | copy-start | bytes 3076
  12.2 2.3 %copy-start.3 = (s32[256]{0:T(256)S(1)}, s32[256]{0:T(256)}, u32[]{:S(2)}) copy-start(s32[256]{0:T(256)} %param.13) | copy-start | bytes 3076

commit v3 on v2

--- a/solution.py
+++ b/solution.py
@@ -4,14 +4,15 @@
 from jax.sharding import PartitionSpec as P
 
 
-def smoothed_basis(filter_taps, basis):
+def smoothed_bases(filter_taps, bases):
     reach = filter_taps.shape[0] - 1
-    lines = basis.astype(jnp.float32).T[:, None, :]
-    kernel = filter_taps.astype(jnp.float32)[::-1][None, None, :]
+    lines = jnp.concatenate([b.T for b in bases], axis=0)[:, None, :]
+    kernel = filter_taps[::-1][None, None, :]
     full = lax.conv_general_dilated(
-        lines, kernel, (1,), [(reach, reach)], precision=lax.Precision.HIGHEST
-    )
-    return full[:, 0, :].T
+        lines, kernel, (1,), [(reach, reach)], preferred_element_type=jnp.float32
+    )[:, 0, :].T
+    sizes = [b.shape[1] for b in bases]
+    return [full[:, sum(sizes[:i]) : sum(sizes[: i + 1])] for i in range(len(bases))]
 
 
 def window_blocks(extended, length):
@@ -33,7 +34,8 @@
         sensitivity.astype(jnp.float32) * inst_weight[:, None, None, None], axis=0
     ).astype(jnp.bfloat16)
 
-    col_blocks = window_blocks(smoothed_basis(filter_taps, basis_cols), tile_cols)
+    row_ext, col_ext = smoothed_bases(filter_taps, (basis_rows, basis_cols))
+    col_blocks = window_blocks(col_ext, tile_cols)
     col_shift = (
         jnp.arange(col_tiles, dtype=jnp.int32)[:, None]
         - jnp.arange(col_tiles, dtype=jnp.int32)[None, :]
@@ -47,14 +49,14 @@
     ).reshape(cols_all, col_tiles * ctrl_cols)
     col_hi = col_matrix.astype(jnp.bfloat16)
     col_lo = (col_matrix - col_hi.astype(jnp.float32)).astype(jnp.bfloat16)
-    flat = summed.reshape(local_rows * comps, cols_all)
-    by_cols = jnp.dot(flat, col_hi, preferred_element_type=jnp.float32) + jnp.dot(
-        flat, col_lo, preferred_element_type=jnp.float32
+    by_cols = jnp.einsum("rkc,cn->rkn", summed, col_hi, preferred_element_type=jnp.float32)
+    by_cols = by_cols + jnp.einsum(
+        "rkc,cn->rkn", summed, col_lo, preferred_element_type=jnp.float32
     )
     by_cols = by_cols.reshape(local_rows, comps * col_tiles * ctrl_cols)
 
     assert local_rows == tile_rows
-    row_blocks = window_blocks(smoothed_basis(filter_taps, basis_rows), tile_rows)[::-1]
+    row_blocks = window_blocks(row_ext, tile_rows)[::-1]
     row_matrix = row_blocks.transpose(0, 2, 1).reshape(3 * ctrl_rows, local_rows)
     parts = jnp.dot(row_matrix, by_cols, precision=lax.Precision.HIGHEST)
     parts = parts.reshape(3, ctrl_rows, comps, col_tiles, ctrl_cols)
@@ -69,8 +71,10 @@
     pick = rel_row * col_tiles + tile_of_slot % col_tiles
     mine = (rel_row >= 0) & (rel_row <= 2)
     outgoing = jnp.where(mine[:, None], parts[jnp.clip(pick, 0, 3 * col_tiles - 1)], 0.0)
+    outgoing = outgoing.astype(jnp.bfloat16).reshape(slots, comps * ctrl_rows * ctrl_cols)
     incoming = lax.all_to_all(outgoing, ("grp", "tile"), 0, 0, tiled=True)
-    return jnp.sum(incoming, axis=0).reshape(1, comps, ctrl_rows * ctrl_cols)
+    total = jnp.sum(incoming.astype(jnp.float32), axis=0)
+    return total.reshape(1, comps, ctrl_rows * ctrl_cols)
 
 
 def solution(mesh):

time: 59 us -> 52.2 us (0.88)
  blocking collectives: 41 us -> 33.6 us
  matrix products: 7.5 us -> 5.04 us
  other arithmetic: 1.62 us -> 3.26 us
  local copies, waits for them, and re-layouts: 8.5 us -> 9.93 us
    all_to_all x1, blocking collectives: 41 us -> 33.6 us  [local(): incoming = lax.all_to_all(outgoing, ('grp', 'tile'), 0, 0, tiled=True)]
    gather x1 -> x2, local copies, waits for them, and re-layouts: 0.63 us -> 5.66 us  [local(): col_blocks[jnp.clip(col_shift, 0, 2)].transpose(0, 2, 1, 3)]
    conv_general_dilated x2 -> x1, matrix products: 4.93 us -> 2.47 us  [smoothed_bases(): lax.conv_general_dilated(lines, kernel, (1,), [(reach, reach)], preferred...]
    convert_element_type x4 -> x1, local copies, waits for them, and re-layouts: 1.72 us -> 0.51 us  [local(): outgoing.astype(jnp.bfloat16).reshape(slots, comps * ctrl_rows * ctrl_cols)]
    broadcast_in_dim x2 -> x1, local copies, waits for them, and re-layouts: 0.94 us -> 0.13 us  [smoothed_bases(): lines = jnp.concatenate([b.T for b in bases], axis=0)[:, None, :]]
    select_n x1 -> x0, local copies, waits for them, and re-layouts: 0.81 us -> none  [local(): jnp.where(mine[:, None], parts[jnp.clip(pick, 0, 3 * col_tiles - 1)], 0.0)]
    convert_element_type x2, other arithmetic: 0.27 us -> 1.05 us  [local(): outgoing.astype(jnp.bfloat16).reshape(slots, comps * ctrl_rows * ctrl_cols)]
    broadcast_in_dim x0 -> x1, other arithmetic: none -> 0.71 us  [smoothed_bases(): lines = jnp.concatenate([b.T for b in bases], axis=0)[:, None, :]]
where the time goes in v3:
time: 52.2 us; the launch traced here: 52 us
  blocking collectives  33.6 us (64%)
  local copies, waits for them, and re-layouts  9.93 us (19%)
  matrix products  5.04 us (10%)
  other arithmetic  3.26 us (6%)
    all_to_all x1, blocking collectives, local(): incoming = lax.all_to_all(outgoing, ('grp', 'tile'), 0, 0, tiled=True)  33.6 us
    gather x2, local copies, waits for them, and re-layouts, local(): col_blocks[jnp.clip(col_shift, 0, 2)].transpose(0, 2, 1, 3)  5.66 us
    conv_general_dilated x1, matrix products, smoothed_bases(): lax.conv_general_dilated(lines, kernel, (1,), [(reach, reach)], preferred...  2.47 us
    dot_general x1, matrix products, local(): parts = jnp.dot(row_matrix, by_cols, precision=lax.Precision.HIGHEST)  1.82 us
    gather x1, local copies, waits for them, and re-layouts, local(): parts[jnp.clip(pick, 0, 3 * col_tiles - 1)]  1.19 us
    convert_element_type x2, other arithmetic, local(): outgoing.astype(jnp.bfloat16).reshape(slots, comps * ctrl_rows * ctrl_cols)  1.05 us

profile of v3, /device:TPU:1, one launch (start us, length us, event | category | flops | bytes accessed | tf_op | source)
XLA Modules:
  0.0 52.0 jit_solution(10626634667711856585)
XLA Ops:
  0.0 0.7 %maximum_bitcast_fusion = bf16[32,1,128]{2,0,1:T(8,128)(2,1)S(1)} fusion(bf16[16,128]{1,0:T(8,128)(2,1)} %bitcast.75, bf16[16,128]{1,0:T(8,128)(2,1)} %bitcast.76), kind=kLoop, calls=%fused_computation.20 | loop fusion | flops 16384 | bytes 16384 | tf_op jit(solution)/shard_map/broadcast_in_dim | solution.py:9
  0.7 0.1 copy.24
  0.9 0.9 %reshape.232 = bf16[1,1,129]{1,0,2:T(2,128)(2,1)S(1)} reshape(bf16[129]{0:T(256)(128)(2,1)} %param.9) | data formatting | bytes 516 | tf_op jit(solution)/shard_map/reshape.34
  1.7 2.5 %fusion.15 = f32[32,1,256]{0,1,2:T(1,128)S(1)} fusion(bf16[1,1,129]{1,0,2:T(2,128)(2,1)S(1)} %reshape.232, bf16[32,1,128]{0,1,2:T(2,128)(2,1)S(1)} %copy.24), kind=kOutput, calls=%fused_computation.40 | convolution fusion | flops 1056768 | bytes 41218 | tf_op jit(solution)/shard_map/conv_general_dilated | solution.py:11
  4.2 0.1 fusion.14
  4.3 0.1 reshape.213
  4.4 2.7 %gather_fusion = f32[64,128,16]{2,1,0:T(8,128)} fusion(f32[3,128,16]{2,1,0:T(8,128)S(1)} %bitcast.66, s32[1024]{0:T(1024)S(1)} %pad_clamp_fusion.1), kind=kCustom, calls=%fused_computation | custom fusion | bytes 1048832 | tf_op jit(solution)/shard_map/gather | solution.py:47
  7.2 0.0 copy-start
  7.2 0.0 copy-start.3
  7.2 2.9 %copy.26 = f32[8,8,128,16]{2,0,3,1:T(8,128)S(1)} copy(f32[8,8,128,16]{3,2,1,0:T(8,128)} %bitcast.67) | data formatting | bytes 1048576 | tf_op jit(solution)/shard_map/gather | solution.py:47
  10.1 0.1 broadcast_select_fusion
  10.2 0.0 copy-done
  10.2 0.0 copy-done.3
  10.2 0.0 copy-start.1
  10.2 0.0 copy-start.2
  10.2 0.4 multiply_reduce_fusion
  10.7 0.4 fusion.3
  11.1 0.4 convolution_add_fusion
  11.5 0.1 copy.25
  11.5 1.8 %convolution_bitcast_fusion = bf16[3,8,3,16,16]{4,3,1,2,0:T(8,128)(2,1)S(1)} fusion(f32[3,8,16,128,1]{3,2,1,0,4:T(8,128)S(1)} %bitcast.71, f32[3,128,16]{1,2,0:T(8,128)S(1)} %rev.4), kind=kOutput, calls=%fused_computation.3 | convolution fusion | flops 28311552 | bytes 258048 | tf_op jit(solution)/shard_map/dot_general | solution.py:61
  13.4 0.3 reshape.209
  13.7 0.0 copy-done.1
  13.7 0.0 copy-done.2
  13.7 0.2 select_reduce_fusion
  13.9 1.2 %gather_fusion.1 = bf16[256,768]{1,0:T(8,128)(2,1)S(1)} fusion(bf16[24,768]{1,0:T(8,128)(2,1)S(1)} %reshape.209, s32[1024]{0:T(1024)S(1)} %pad_clamp_fusion), kind=kCustom, calls=%fused_computation.1 | custom fusion | bytes 787456 | tf_op jit(solution)/shard_map/gather | solution.py:73
  15.1 0.1 fusion
  15.3 0.5 broadcast.279
  15.8 0.9 %reduce.1 = bf16[256,768]{1,0:T(8,128)(2,1)S(1)} reduce(bf16[256,1,768]{2,0,1:T(8,128)(2,1)S(1)} %fusion, bf16[]{:T(256)} %broadcast.279), dimensions={1}, to_apply=%copy.28.reduce_sub_computation | reduce | bytes 786434 | tf_op jit(solution)/shard_map/convert_element_type | solution.py:74
  16.7 0.1 reshape.233
  16.8 33.6 %all_to_all.6 = bf16[256,2,384]{2,1,0:T(2,128)(2,1)S(1)} all-to-all(bf16[256,2,384]{2,1,0:T(2,128)(2,1)S(1)} %reshape.233), channel_id=1, replica_groups=mesh['grp'=8,'tile'=32] {'grp','tile'}, dimensions={0} | all-to-all | bytes 786432 | tf_op jit(solution)/shard_map/all_to_all | solution.py:75
  50.4 0.3 reshape.234
  50.7 0.7 %convert_reduce_fusion = f32[768]{0:T(1024)S(1)} fusion(bf16[256,1,768]{2,1,0:T(2,128)(2,1)S(1)} %reshape.234), kind=kLoop, calls=%fused_computation.7 | loop fusion | flops 392448 | bytes 396288 | tf_op jit(solution)/shard_map/reduce_sum | solution.py:76
  51.5 0.6 %reshape.210 = f32[1,3,256]{2,0,1:T(1,128)} reshape(f32[768]{0:T(1024)S(1)} %convert_reduce_fusion) | data formatting | bytes 6144 | tf_op jit(solution)/shard_map/reshape | solution.py:77
  (10 shorter events, 0.1 us)
Async XLA Ops:
  7.2 3.0 %copy-start = (bf16[2,128,3,1024]{3,1,2,0:T(8,128)(2,1)S(1)}, bf16[2,128,3,1024]{3,1,2,0:T(8,128)(2,1)}, u32[]{:S(2)}) copy-start(bf16[2,128,3,1024]{3,1,2,0:T(8,128)(2,1)} %param.7) | copy-start | bytes 4718596
  7.2 3.1 %copy-start.3 = (f32[2]{0:T(128)S(1)}, f32[2]{0:T(128)}, u32[]{:S(2)}) copy-start(f32[2]{0:T(128)} %param.8) | copy-start | bytes 28
  10.2 3.4 %copy-start.1 = (s32[256,1]{0,1:T(1,128)S(1)}, s32[256,1]{0,1:T(1,128)}, u32[]{:S(2)}) copy-start(s32[256,1]{0,1:T(1,128)} %param.12) | copy-start | bytes 3076
  10.2 3.4 %copy-start.2 = (s32[256]{0:T(256)S(1)}, s32[256]{0:T(256)}, u32[]{:S(2)}) copy-start(s32[256]{0:T(256)} %param.13) | copy-start | bytes 3076

commit v4 on v2

v4 whole, which is shorter than its diff:
```python
import functools

import jax
import jax.numpy as jnp
from jax import lax
from jax.experimental import pallas as pl
from jax.experimental.pallas import tpu as pltpu
from jax.sharding import PartitionSpec as P


def fold_kernel(half, w_ref, taps_ref, bases_ref, sens_ref, out_ref, ct_ref):
    insts, comps, rows, cols = sens_ref.shape
    ctrl = bases_ref.shape[0] // 2
    tile = bases_ref.shape[1]
    col_tiles = cols // tile
    period = taps_ref.shape[1]

    base = jnp.broadcast_to(taps_ref[...], (tile, period))
    blocks = []
    for b in range(3):
        rolled = pltpu.roll(base, (-(tile * (b - 1) + half)) % period, 1, stride=1, stride_axis=0)
        blocks.append(rolled[:, :tile])
    toeplitz = jnp.concatenate(blocks, axis=1).astype(jnp.bfloat16)
    smoothed = jnp.dot(bases_ref[...], toeplitz, preferred_element_type=jnp.float32)

    ct_ref[...] = jnp.zeros(ct_ref.shape, jnp.float32)
    for y in range(col_tiles):
        for cb in range(max(0, y - 1), min(col_tiles, y + 2)):
            b = cb - y + 1
            ct_ref[ctrl * y : ctrl * (y + 1), tile * cb : tile * (cb + 1)] = smoothed[
                :ctrl, tile * b : tile * (b + 1)
            ]
    ct = ct_ref[...]
    ct_hi = ct.astype(jnp.bfloat16)
    ct_lo = (ct - ct_hi.astype(jnp.float32)).astype(jnp.bfloat16)
    rows_matrix = jnp.concatenate(
        [smoothed[ctrl:, tile * (2 - d) : tile * (3 - d)] for d in range(3)], axis=0
    )
    nt = (((1,), (1,)), ((), ()))
    for k in range(comps):
        summed = (sens_ref[0, k].astype(jnp.float32) * w_ref[0]).astype(jnp.float32)
        for i in range(1, insts):
            summed = summed + sens_ref[i, k].astype(jnp.float32) * w_ref[i]
        summed = summed.astype(jnp.bfloat16)
        by_cols = lax.dot_general(summed, ct_hi, nt, preferred_element_type=jnp.float32)
        by_cols = by_cols + lax.dot_general(summed, ct_lo, nt, preferred_element_type=jnp.float32)
        out_ref[k] = jnp.dot(
            rows_matrix, by_cols, precision=lax.Precision.HIGHEST, preferred_element_type=jnp.float32
        )


def local(sensitivity, inst_weight, filter_taps, basis_rows, basis_cols, box_table, owner_perm):
    tile_rows, ctrl_rows = basis_rows.shape
    tile_cols, ctrl_cols = basis_cols.shape
    insts, local_rows, comps, cols_all = sensitivity.shape
    col_tiles = cols_all // tile_cols
    slots = owner_perm.shape[0]
    assert local_rows == tile_rows and tile_rows == tile_cols and ctrl_rows == ctrl_cols

    period = 4 * tile_rows
    taps_row = jnp.pad(filter_taps.astype(jnp.float32), (0, period - filter_taps.shape[0]))[None, :]
    bases = jnp.concatenate([basis_cols.T, basis_rows.T], axis=0)
    parts = pl.pallas_call(
        functools.partial(fold_kernel, (filter_taps.shape[0] - 1) // 2),
        out_shape=jax.ShapeDtypeStruct((comps, 3 * ctrl_rows, col_tiles * ctrl_cols), jnp.float32),
        in_specs=[
            pl.BlockSpec(memory_space=pltpu.SMEM),
            pl.BlockSpec(memory_space=pltpu.VMEM),
            pl.BlockSpec(memory_space=pltpu.VMEM),
            pl.BlockSpec(memory_space=pltpu.VMEM),
        ],
        out_specs=pl.BlockSpec(memory_space=pltpu.VMEM),
        scratch_shapes=[pltpu.VMEM((col_tiles * ctrl_cols, cols_all), jnp.float32)],
    )(inst_weight, taps_row, bases, jnp.transpose(sensitivity, (0, 2, 1, 3)))
    parts = parts.reshape(comps, 3, ctrl_rows, col_tiles, ctrl_cols)
    parts = parts.transpose(1, 3, 0, 2, 4).reshape(3 * col_tiles, comps * ctrl_rows * ctrl_cols)

    tiles = jnp.arange(box_table.shape[0], dtype=jnp.int32)
    tile_of_slot = jnp.sum(
        jnp.where(box_table[:, 0][None, :] == owner_perm[:, None], tiles[None, :], 0), axis=1
    )
    here = lax.axis_index("tile")
    rel_row = tile_of_slot // col_tiles - here + 1
    pick = rel_row * col_tiles + tile_of_slot % col_tiles
    mine = (rel_row >= 0) & (rel_row <= 2)
    outgoing = jnp.where(mine[:, None], parts[jnp.clip(pick, 0, 3 * col_tiles - 1)], 0.0)
    outgoing = outgoing.astype(jnp.bfloat16)
    incoming = lax.all_to_all(outgoing, ("grp", "tile"), 0, 0, tiled=True)
    total = jnp.sum(incoming.astype(jnp.float32), axis=0)
    return total.reshape(1, comps, ctrl_rows * ctrl_cols)


def solution(mesh):
    placed = (P("grp", "tile", None, None), P("grp"), P(), P(), P(), P(), P())
    return jax.shard_map(
        local, mesh=mesh, in_specs=placed, out_specs=P(("grp", "tile"), None, None), check_vma=False
    )
```

time: 59 us -> 46.8 us (0.79)
  matrix products: 7.5 us -> 0 us
  blocking collectives: 41 us -> 33.6 us
  local copies, waits for them, and re-layouts: 8.5 us -> 4.11 us
  Pallas kernels: 0 us -> 3.61 us
  other arithmetic: 1.62 us -> 5.22 us
    all_to_all x1, blocking collectives: 41 us -> 33.6 us  [local(): incoming = lax.all_to_all(outgoing, ('grp', 'tile'), 0, 0, tiled=True)]
    conv_general_dilated x2 -> x0, matrix products: 4.93 us -> none  [smoothed_basis(): lax.conv_general_dilated(lines, kernel, (1,), [(reach, reach)], precision...]
    pallas_call x0 -> x1, Pallas kernels: none -> 3.61 us  [local(): pl.pallas_call(functools.partial(fold_kernel, (filter_taps.shape[0] - 1)...]
    dot_general x3 -> x0, matrix products: 2.57 us -> none  [the longest x1 1.82 us: local(): parts = jnp.dot(row_matrix, by_cols, precision=lax.Precision.HIGHEST)]
    concatenate x0 -> x1, other arithmetic: none -> 1.3 us  [local(): bases = jnp.concatenate([basis_cols.T, basis_rows.T], axis=0)]
    broadcast_in_dim x0 -> x1, other arithmetic: none -> 1.24 us  [local(): jnp.pad(filter_taps.astype(jnp.float32), (0, period - filter_taps.shape[0]))]
    convert_element_type x4 -> x1, local copies, waits for them, and re-layouts: 1.72 us -> 0.51 us  [local(): outgoing = outgoing.astype(jnp.bfloat16)]
    broadcast_in_dim x2 -> x0, local copies, waits for them, and re-layouts: 0.94 us -> none  [smoothed_basis(): lines = basis.astype(jnp.float32).T[:, None, :]]
where the time goes in v4:
time: 46.8 us; the launch traced here: 46.6 us
  blocking collectives  33.6 us (72%)
  other arithmetic  5.22 us (11%)
  local copies, waits for them, and re-layouts  4.11 us (9%)
  Pallas kernels  3.61 us (8%)
    all_to_all x1, blocking collectives, local(): incoming = lax.all_to_all(outgoing, ('grp', 'tile'), 0, 0, tiled=True)  33.6 us
    pallas_call x1, Pallas kernels, local(): pl.pallas_call(functools.partial(fold_kernel, (filter_taps.shape[0] - 1)...  3.61 us
    concatenate x1, other arithmetic, local(): bases = jnp.concatenate([basis_cols.T, basis_rows.T], axis=0)  1.3 us
    broadcast_in_dim x1, other arithmetic, local(): jnp.pad(filter_taps.astype(jnp.float32), (0, period - filter_taps.shape[0]))  1.24 us
    gather x1, local copies, waits for them, and re-layouts, local(): parts[jnp.clip(pick, 0, 3 * col_tiles - 1)]  1.19 us
    reshape x1, local copies, waits for them, and re-layouts, local(): parts = parts.reshape(comps, 3, ctrl_rows, col_tiles, ctrl_cols)  1.11 us
    convert_element_type x2, other arithmetic, local(): outgoing = outgoing.astype(jnp.bfloat16)  1.05 us

profile of v4, /device:TPU:1, one launch (start us, length us, event | category | flops | bytes accessed | tf_op | source)
XLA Modules:
  0.0 46.6 jit_solution(1457381481162245572)
XLA Ops:
  0.0 0.9 %select_reduce_fusion = s32[256]{0:T(256)S(1)} fusion(s32[256]{0:T(256)} %bitcast.21, s32[256]{0:T(256)} %param.13), kind=kLoop, calls=%fused_computation.4 | loop fusion | flops 196352 | bytes 3072 | tf_op jit(solution)/shard_map/reduce_sum | solution.py:79
  0.9 1.2 %pad_convert_fusion = f32[512]{0:T(512)} fusion(bf16[129]{0:T(256)(128)(2,1)} %param.9), kind=kLoop, calls=%fused_computation.19 | loop fusion | flops 512 | bytes 2306 | tf_op jit(solution)/shard_map/broadcast_in_dim | solution.py:61
  2.2 1.3 %pad_maximum_fusion.bases_ref = bf16[32,128]{1,0:T(8,128)(2,1)} fusion(bf16[16,128]{1,0:T(8,128)(2,1)} %bitcast.19, bf16[16,128]{1,0:T(8,128)(2,1)} %bitcast.20), kind=kLoop, calls=%fused_computation.5 | loop fusion | flops 16384 | bytes 16384 | tf_op jit(solution)/shard_map/concatenate | solution.py:62
  3.5 3.6 %shard_map.73 = f32[3,48,128]{2,1,0:T(8,128)} custom-call(f32[2]{0:T(128)} %w_ref.1, f32[1,512]{1,0:T(1,128)} %bitcast.17, bf16[32,128]{1,0:T(8,128)(2,1)} %pad_maximum_fusion.bases_ref, bf16[2,3,128,1024]{3,2,1,0:T(8,128)(2,1)} %bitcast.14), custom_call_target="tpu_custom_call" | custom-call | tf_op jit(solution)/shard_map/pallas_call | solution.py:63
  7.1 1.1 %reshape.139 = bf16[3,3,16,8,16]{4,3,2,1,0:T(8,128)(2,1)S(1)} reshape(f32[3,48,128]{2,1,0:T(8,128)} %shard_map.73) | data formatting | bytes 110592 | tf_op jit(solution)/shard_map/reshape | solution.py:75
  8.2 0.3 reshape.140
  8.5 1.2 %gather_fusion = bf16[256,768]{1,0:T(8,128)(2,1)S(1)} fusion(bf16[24,768]{1,0:T(8,128)(2,1)S(1)} %reshape.140, s32[1024]{0:T(1024)S(1)} %pad_clamp_fusion), kind=kCustom, calls=%fused_computation | custom fusion | bytes 787456 | tf_op jit(solution)/shard_map/gather | solution.py:86
  9.7 0.1 fusion
  9.8 0.5 %broadcast.203 = bf16[]{:T(256)} broadcast(bf16[]{:T(256)} %constant.70), dimensions={} | broadcast | bytes 4 | tf_op jit(solution)/shard_map/convert_element_type | solution.py:87
  10.3 0.9 %reduce.1 = bf16[256,768]{1,0:T(8,128)(2,1)S(1)} reduce(bf16[256,1,768]{2,0,1:T(8,128)(2,1)S(1)} %fusion, bf16[]{:T(256)} %broadcast.203), dimensions={1}, to_apply=%copy.13.reduce_sub_computation | reduce | bytes 786434 | tf_op jit(solution)/shard_map/convert_element_type | solution.py:87
  11.3 0.1 reshape.151
  11.4 33.6 %all_to_all.6 = bf16[256,2,384]{2,1,0:T(2,128)(2,1)S(1)} all-to-all(bf16[256,2,384]{2,1,0:T(2,128)(2,1)S(1)} %reshape.151), channel_id=1, replica_groups=mesh['grp'=8,'tile'=32] {'grp','tile'}, dimensions={0} | all-to-all | bytes 786432 | tf_op jit(solution)/shard_map/all_to_all | solution.py:88
  45.0 0.3 reshape.152
  45.3 0.7 %convert_reduce_fusion = f32[768]{0:T(1024)S(1)} fusion(bf16[256,1,768]{2,1,0:T(2,128)(2,1)S(1)} %reshape.152), kind=kLoop, calls=%fused_computation.3 | loop fusion | flops 392448 | bytes 396288 | tf_op jit(solution)/shard_map/reduce_sum | solution.py:89
  46.0 0.6 %reshape.141 = f32[1,3,256]{2,0,1:T(1,128)} reshape(f32[768]{0:T(1024)S(1)} %convert_reduce_fusion) | data formatting | bytes 6144 | tf_op jit(solution)/shard_map/reshape | solution.py:90
  (4 shorter events, 0.1 us)

commit v5 on v4

--- a/solution.py
+++ b/solution.py
@@ -8,20 +8,23 @@
 from jax.sharding import PartitionSpec as P
 
 
-def fold_kernel(half, w_ref, taps_ref, bases_ref, sens_ref, out_ref, ct_ref):
+def fold_kernel(w_ref, taps_ref, cols_ref, rows_ref, sens_ref, out_ref, ct_ref, taps_row):
     insts, comps, rows, cols = sens_ref.shape
-    ctrl = bases_ref.shape[0] // 2
-    tile = bases_ref.shape[1]
+    ctrl, tile = cols_ref.shape
     col_tiles = cols // tile
-    period = taps_ref.shape[1]
+    period = taps_row.shape[1]
+    half = (taps_ref.shape[1] - 1) // 2
 
-    base = jnp.broadcast_to(taps_ref[...], (tile, period))
+    taps_row[...] = jnp.zeros(taps_row.shape, jnp.float32)
+    taps_row[:, : taps_ref.shape[1]] = taps_ref[...].astype(jnp.float32)
+    base = jnp.broadcast_to(taps_row[...], (tile, period))
     blocks = []
     for b in range(3):
         rolled = pltpu.roll(base, (-(tile * (b - 1) + half)) % period, 1, stride=1, stride_axis=0)
         blocks.append(rolled[:, :tile])
     toeplitz = jnp.concatenate(blocks, axis=1).astype(jnp.bfloat16)
-    smoothed = jnp.dot(bases_ref[...], toeplitz, preferred_element_type=jnp.float32)
+    bases = jnp.concatenate([cols_ref[...], rows_ref[...]], axis=0)
+    smoothed = jnp.dot(bases, toeplitz, preferred_element_type=jnp.float32)
 
     ct_ref[...] = jnp.zeros(ct_ref.shape, jnp.float32)
     for y in range(col_tiles):
@@ -46,7 +49,7 @@
         by_cols = by_cols + lax.dot_general(summed, ct_lo, nt, preferred_element_type=jnp.float32)
         out_ref[k] = jnp.dot(
             rows_matrix, by_cols, precision=lax.Precision.HIGHEST, preferred_element_type=jnp.float32
-        )
+        ).astype(out_ref.dtype)
 
 
 def local(sensitivity, inst_weight, filter_taps, basis_rows, basis_cols, box_table, owner_perm):
@@ -58,20 +61,22 @@
     assert local_rows == tile_rows and tile_rows == tile_cols and ctrl_rows == ctrl_cols
 
     period = 4 * tile_rows
-    taps_row = jnp.pad(filter_taps.astype(jnp.float32), (0, period - filter_taps.shape[0]))[None, :]
-    bases = jnp.concatenate([basis_cols.T, basis_rows.T], axis=0)
     parts = pl.pallas_call(
-        functools.partial(fold_kernel, (filter_taps.shape[0] - 1) // 2),
-        out_shape=jax.ShapeDtypeStruct((comps, 3 * ctrl_rows, col_tiles * ctrl_cols), jnp.float32),
-        in_specs=[
-            pl.BlockSpec(memory_space=pltpu.SMEM),
-            pl.BlockSpec(memory_space=pltpu.VMEM),
-            pl.BlockSpec(memory_space=pltpu.VMEM),
-            pl.BlockSpec(memory_space=pltpu.VMEM),
+        fold_kernel,
+        out_shape=jax.ShapeDtypeStruct((comps, 3 * ctrl_rows, col_tiles * ctrl_cols), jnp.bfloat16),
+        in_specs=[pl.BlockSpec(memory_space=pltpu.SMEM)] + [pl.BlockSpec(memory_space=pltpu.VMEM)] * 4,
+        out_specs=pl.BlockSpec(memory_space=pltpu.VMEM),
+        scratch_shapes=[
+            pltpu.VMEM((col_tiles * ctrl_cols, cols_all), jnp.float32),
+            pltpu.VMEM((1, period), jnp.float32),
         ],
-        out_specs=pl.BlockSpec(memory_space=pltpu.VMEM),
-        scratch_shapes=[pltpu.VMEM((col_tiles * ctrl_cols, cols_all), jnp.float32)],
-    )(inst_weight, taps_row, bases, jnp.transpose(sensitivity, (0, 2, 1, 3)))
+    )(
+        inst_weight,
+        filter_taps[None, :],
+        basis_cols.T,
+        basis_rows.T,
+        jnp.transpose(sensitivity, (0, 2, 1, 3)),
+    )
     parts = parts.reshape(comps, 3, ctrl_rows, col_tiles, ctrl_cols)
     parts = parts.transpose(1, 3, 0, 2, 4).reshape(3 * col_tiles, comps * ctrl_rows * ctrl_cols)
 
@@ -82,12 +87,15 @@
     here = lax.axis_index("tile")
     rel_row = tile_of_slot // col_tiles - here + 1
     pick = rel_row * col_tiles + tile_of_slot % col_tiles
-    mine = (rel_row >= 0) & (rel_row <= 2)
-    outgoing = jnp.where(mine[:, None], parts[jnp.clip(pick, 0, 3 * col_tiles - 1)], 0.0)
-    outgoing = outgoing.astype(jnp.bfloat16)
+    select = (pick[:, None] == jnp.arange(3 * col_tiles, dtype=jnp.int32)[None, :]).astype(
+        jnp.bfloat16
+    )
+    outgoing = jnp.dot(select, parts, preferred_element_type=jnp.float32).astype(jnp.bfloat16)
     incoming = lax.all_to_all(outgoing, ("grp", "tile"), 0, 0, tiled=True)
-    total = jnp.sum(incoming.astype(jnp.float32), axis=0)
-    return total.reshape(1, comps, ctrl_rows * ctrl_cols)
+    total = jnp.sum(
+        incoming.astype(jnp.float32).reshape(slots, comps, ctrl_rows * ctrl_cols), axis=0
+    )
+    return total[None]
 
 
 def solution(mesh):

time: 46.8 us -> 43.7 us (0.934)
  other arithmetic: 5.22 us -> 1.83 us
    broadcast_in_dim x0 -> x2, local copies, waits for them, and re-layouts: none -> 1.84 us  [the longest x1 1.25 us: local(): filter_taps[None, :]]
    concatenate x1 -> x0, other arithmetic: 1.3 us -> none  [local(): bases = jnp.concatenate([basis_cols.T, basis_rows.T], axis=0)]
    broadcast_in_dim x1 -> x0, other arithmetic: 1.24 us -> none  [local(): jnp.pad(filter_taps.astype(jnp.float32), (0, period - filter_taps.shape[0]))]
    gather x1 -> x0, local copies, waits for them, and re-layouts: 1.19 us -> none  [local(): parts[jnp.clip(pick, 0, 3 * col_tiles - 1)]]
    convert_element_type x2 -> x0, other arithmetic: 1.05 us -> none  [local(): outgoing = outgoing.astype(jnp.bfloat16)]
    all_to_all x0 -> x1, other arithmetic: none -> 0.92 us  [local(): incoming = lax.all_to_all(outgoing, ('grp', 'tile'), 0, 0, tiled=True)]
    reduce_sum x1, other arithmetic: 0.87 us -> 0.18 us  [local(): jnp.sum(jnp.where(box_table[:, 0][None, :] == owner_perm[:, None], tiles[...]
    reshape x1 -> x0, local copies, waits for them, and re-layouts: 0.59 us -> none  [local(): return total.reshape(1, comps, ctrl_rows * ctrl_cols)]
where the time goes in v5:
time: 43.7 us; the launch traced here: 43.5 us
  blocking collectives  33.6 us (77%)
  local copies, waits for them, and re-layouts  4.05 us (9%)
  Pallas kernels  3.62 us (8%)
  other arithmetic  1.83 us (4%)
    all_to_all x1, blocking collectives, local(): incoming = lax.all_to_all(outgoing, ('grp', 'tile'), 0, 0, tiled=True)  33.6 us
    pallas_call x1, Pallas kernels, local(): pl.pallas_call(fold_kernel, out_shape=jax.ShapeDtypeStruct((comps, 3 * ct...  3.62 us
    broadcast_in_dim x1, local copies, waits for them, and re-layouts, local(): filter_taps[None, :]  1.25 us
    reshape x2, local copies, waits for them, and re-layouts, local(): parts = parts.reshape(comps, 3, ctrl_rows, col_tiles, ctrl_cols)  1.03 us
    all_to_all x1, other arithmetic, local(): incoming = lax.all_to_all(outgoing, ('grp', 'tile'), 0, 0, tiled=True)  0.92 us

profile of v5, /device:TPU:1, one launch (start us, length us, event | category | flops | bytes accessed | tf_op | source)
XLA Modules:
  0.0 43.5 jit_solution(13701456800133707031)
XLA Ops:
  0.0 0.0 copy-start.1
  0.0 0.0 copy-start
  0.0 1.2 %broadcast_in_dim.24.taps_ref = bf16[1,129]{1,0:T(2,128)(2,1)} reshape(bf16[129]{0:T(256)(128)(2,1)} %param.9) | data formatting | bytes 516 | tf_op jit(solution)/shard_map/broadcast_in_dim | solution.py:75
  1.3 3.6 %shard_map.73 = bf16[3,48,128]{2,1,0:T(8,128)(2,1)} custom-call(f32[2]{0:T(128)} %w_ref.1, bf16[1,129]{1,0:T(2,128)(2,1)} %broadcast_in_dim.24.taps_ref, bf16[16,128]{1,0:T(8,128)(2,1)} %bitcast.14, bf16[16,128]{1,0:T(8,128)(2,1)} %bitcast.15, bf16[2,3,128,1024]{3,2,1,0:T(8,128)(2,1)} %bitcast.12), custom_call_target="tpu_custom_call" | custom-call | tf_op jit(solution)/shard_map/pallas_call | solution.py:64
  4.9 1.0 %reshape.46 = bf16[3,3,16,8,16]{4,3,2,1,0:T(8,128)(2,1)S(1)} reshape(bf16[3,48,128]{2,1,0:T(8,128)(2,1)} %shard_map.73) | data formatting | bytes 73728 | tf_op jit(solution)/shard_map/reshape | solution.py:80
  5.9 0.3 reshape.47
  6.2 0.0 copy-done.1
  6.2 0.0 copy-done
  6.2 0.2 select_reduce_fusion
  6.4 0.3 fusion
  6.7 0.5 %broadcast.74 = bf16[]{:T(256)} broadcast(bf16[]{:T(256)} %constant.46), dimensions={} | broadcast | bytes 4 | tf_op jit(solution)/shard_map/all_to_all | solution.py:94
  7.2 0.9 %reduce.1 = bf16[256,768]{1,0:T(8,128)(2,1)S(1)} reduce(bf16[256,1,768]{2,0,1:T(8,128)(2,1)S(1)} %fusion, bf16[]{:T(256)} %broadcast.74), dimensions={1}, to_apply=%copy.12.reduce_sub_computation | reduce | bytes 786434 | tf_op jit(solution)/shard_map/all_to_all | solution.py:94
  8.1 0.1 reshape.48
  8.2 33.6 %all_to_all.9 = bf16[256,2,384]{2,1,0:T(2,128)(2,1)S(1)} all-to-all(bf16[256,2,384]{2,1,0:T(2,128)(2,1)S(1)} %reshape.48), channel_id=1, replica_groups=mesh['grp'=8,'tile'=32] {'grp','tile'}, dimensions={0} | all-to-all | bytes 786432 | tf_op jit(solution)/shard_map/all_to_all | solution.py:94
  41.9 0.3 reshape.49
  42.2 0.7 %convert_reduce_fusion = f32[768]{0:T(1024)S(1)} fusion(bf16[256,1,768]{2,1,0:T(2,128)(2,1)S(1)} %reshape.49), kind=kLoop, calls=%fused_computation.2 | loop fusion | flops 392448 | bytes 396288 | tf_op jit(solution)/shard_map/reduce_sum | solution.py:95
  42.9 0.6 %broadcast_in_dim.25 = f32[1,3,256]{2,0,1:T(1,128)} reshape(f32[768]{0:T(1024)S(1)} %convert_reduce_fusion) | data formatting | bytes 6144 | tf_op jit(solution)/shard_map/broadcast_in_dim | solution.py:98
  (2 shorter events, 0.1 us)
Async XLA Ops:
  0.0 6.2 %copy-start.1 = (s32[256]{0:T(256)S(1)}, s32[256]{0:T(256)}, u32[]{:S(2)}) copy-start(s32[256]{0:T(256)} %param.13) | copy-start | bytes 3076
  0.0 6.2 %copy-start = (s32[256,1]{0,1:T(1,128)S(1)}, s32[256,1]{0,1:T(1,128)}, u32[]{:S(2)}) copy-start(s32[256,1]{0,1:T(1,128)} %param.12) | copy-start | bytes 3076

commit v6 on v5

--- a/solution.py
+++ b/solution.py
@@ -8,15 +8,17 @@
 from jax.sharding import PartitionSpec as P
 
 
-def fold_kernel(w_ref, taps_ref, cols_ref, rows_ref, sens_ref, out_ref, ct_ref, taps_row):
+def fold_kernel(
+    w_ref, taps_ref, cols_ref, rows_ref, sens_ref, pick_ref, out_ref, ct_ref, taps_row, parts_ref
+):
     insts, comps, rows, cols = sens_ref.shape
     ctrl, tile = cols_ref.shape
     col_tiles = cols // tile
     period = taps_row.shape[1]
-    half = (taps_ref.shape[1] - 1) // 2
+    half = (taps_ref.shape[0] - 1) // 2
 
     taps_row[...] = jnp.zeros(taps_row.shape, jnp.float32)
-    taps_row[:, : taps_ref.shape[1]] = taps_ref[...].astype(jnp.float32)
+    taps_row[:, : taps_ref.shape[0]] = taps_ref[...].astype(jnp.float32)[None, :]
     base = jnp.broadcast_to(taps_row[...], (tile, period))
     blocks = []
     for b in range(3):
@@ -40,6 +42,20 @@
         [smoothed[ctrl:, tile * (2 - d) : tile * (3 - d)] for d in range(3)], axis=0
     )
     nt = (((1,), (1,)), ((), ()))
+    lanes = col_tiles * ctrl
+    block = ctrl * ctrl
+    spread = (
+        lax.broadcasted_iota(jnp.int32, (3 * ctrl, 3 * block), 0)
+        == lax.broadcasted_iota(jnp.int32, (3 * ctrl, 3 * block), 1) // ctrl
+    ).astype(jnp.bfloat16)
+    keep = (
+        lax.broadcasted_iota(jnp.int32, (lanes, 3 * block), 0) % ctrl
+        == lax.broadcasted_iota(jnp.int32, (lanes, 3 * block), 1) % ctrl
+    )
+    gather_y = (
+        lax.broadcasted_iota(jnp.int32, (col_tiles, lanes), 0)
+        == lax.broadcasted_iota(jnp.int32, (col_tiles, lanes), 1) // ctrl
+    ).astype(jnp.bfloat16)
     for k in range(comps):
         summed = (sens_ref[0, k].astype(jnp.float32) * w_ref[0]).astype(jnp.float32)
         for i in range(1, insts):
@@ -47,9 +63,24 @@
         summed = summed.astype(jnp.bfloat16)
         by_cols = lax.dot_general(summed, ct_hi, nt, preferred_element_type=jnp.float32)
         by_cols = by_cols + lax.dot_general(summed, ct_lo, nt, preferred_element_type=jnp.float32)
-        out_ref[k] = jnp.dot(
+        z = jnp.dot(
             rows_matrix, by_cols, precision=lax.Precision.HIGHEST, preferred_element_type=jnp.float32
-        ).astype(out_ref.dtype)
+        )
+        zt = z.T.astype(jnp.bfloat16)
+        wide = jnp.dot(zt, spread, preferred_element_type=jnp.float32)
+        wide = jnp.where(keep, wide, 0.0).astype(jnp.bfloat16)
+        moved = jnp.dot(gather_y, wide, preferred_element_type=jnp.float32).astype(jnp.bfloat16)
+        for d in range(3):
+            parts_ref[col_tiles * d : col_tiles * (d + 1), block * k : block * (k + 1)] = moved[
+                :, block * d : block * (d + 1)
+            ]
+    rows_of_parts = parts_ref.shape[0]
+    select = (
+        pick_ref[...] == lax.broadcasted_iota(jnp.int32, (out_ref.shape[0], rows_of_parts), 1)
+    ).astype(jnp.bfloat16)
+    out_ref[...] = jnp.dot(select, parts_ref[...], preferred_element_type=jnp.float32).astype(
+        out_ref.dtype
+    )
 
 
 def local(sensitivity, inst_weight, filter_taps, basis_rows, basis_cols, box_table, owner_perm):
@@ -61,36 +92,33 @@
     assert local_rows == tile_rows and tile_rows == tile_cols and ctrl_rows == ctrl_cols
 
     period = 4 * tile_rows
-    parts = pl.pallas_call(
+    tiles = jnp.arange(box_table.shape[0], dtype=jnp.int32)
+    tile_of_slot = jnp.sum(
+        jnp.where(box_table[:, 0][None, :] == owner_perm[:, None], tiles[None, :], 0),
+        axis=1,
+        keepdims=True,
+    )
+    here = lax.axis_index("tile")
+    rel_row = tile_of_slot // col_tiles - here + 1
+    pick = rel_row * col_tiles + tile_of_slot % col_tiles
+    outgoing = pl.pallas_call(
         fold_kernel,
-        out_shape=jax.ShapeDtypeStruct((comps, 3 * ctrl_rows, col_tiles * ctrl_cols), jnp.bfloat16),
-        in_specs=[pl.BlockSpec(memory_space=pltpu.SMEM)] + [pl.BlockSpec(memory_space=pltpu.VMEM)] * 4,
+        out_shape=jax.ShapeDtypeStruct((slots, comps * ctrl_rows * ctrl_cols), jnp.bfloat16),
+        in_specs=[pl.BlockSpec(memory_space=pltpu.SMEM)] + [pl.BlockSpec(memory_space=pltpu.VMEM)] * 5,
         out_specs=pl.BlockSpec(memory_space=pltpu.VMEM),
         scratch_shapes=[
             pltpu.VMEM((col_tiles * ctrl_cols, cols_all), jnp.float32),
             pltpu.VMEM((1, period), jnp.float32),
+            pltpu.VMEM((3 * col_tiles, comps * ctrl_rows * ctrl_cols), jnp.bfloat16),
         ],
     )(
         inst_weight,
-        filter_taps[None, :],
+        filter_taps,
         basis_cols.T,
         basis_rows.T,
         jnp.transpose(sensitivity, (0, 2, 1, 3)),
+        pick,
     )
-    parts = parts.reshape(comps, 3, ctrl_rows, col_tiles, ctrl_cols)
-    parts = parts.transpose(1, 3, 0, 2, 4).reshape(3 * col_tiles, comps * ctrl_rows * ctrl_cols)
-
-    tiles = jnp.arange(box_table.shape[0], dtype=jnp.int32)
-    tile_of_slot = jnp.sum(
-        jnp.where(box_table[:, 0][None, :] == owner_perm[:, None], tiles[None, :], 0), axis=1
-    )
-    here = lax.axis_index("tile")
-    rel_row = tile_of_slot // col_tiles - here + 1
-    pick = rel_row * col_tiles + tile_of_slot % col_tiles
-    select = (pick[:, None] == jnp.arange(3 * col_tiles, dtype=jnp.int32)[None, :]).astype(
-        jnp.bfloat16
-    )
-    outgoing = jnp.dot(select, parts, preferred_element_type=jnp.float32).astype(jnp.bfloat16)
     incoming = lax.all_to_all(outgoing, ("grp", "tile"), 0, 0, tiled=True)
     total = jnp.sum(
         incoming.astype(jnp.float32).reshape(slots, comps, ctrl_rows * ctrl_cols), axis=0

time: 43.7 us -> 44.8 us (1.025)
  other arithmetic: 1.83 us -> 4.26 us
  local copies, waits for them, and re-layouts: 4.05 us -> 1.65 us
  Pallas kernels: 3.62 us -> 5.03 us
    pallas_call x1, Pallas kernels: 3.62 us -> 5.03 us  [local(): pl.pallas_call(fold_kernel, out_shape=jax.ShapeDtypeStruct((slots, comps...]
    reshape x3 -> x0, local copies, waits for them, and re-layouts: 1.29 us -> none  [the longest x2 1.03 us: local(): parts = parts.reshape(comps, 3, ctrl_rows, col_tiles, ctrl_cols)]
    broadcast_in_dim x1 -> x0, local copies, waits for them, and re-layouts: 1.25 us -> none  [local(): filter_taps[None, :]]
    all_to_all x1, other arithmetic: 0.92 us -> 1.88 us  [local(): incoming = lax.all_to_all(outgoing, ('grp', 'tile'), 0, 0, tiled=True)]
    add x1, other arithmetic: 0.02 us -> 0.79 us  [local(): pick = rel_row * col_tiles + tile_of_slot % col_tiles]
    reduce_sum x1, other arithmetic: 0.18 us -> 0.87 us  [local(): jnp.sum(jnp.where(box_table[:, 0][None, :] == owner_perm[:, None], tiles[...]
where the time goes in v6:
time: 44.8 us; the launch traced here: 44.6 us
  blocking collectives  33.6 us (75%)
  Pallas kernels  5.03 us (11%)
  other arithmetic  4.26 us (10%)
  local copies, waits for them, and re-layouts  1.65 us (4%)
    all_to_all x1, blocking collectives, local(): incoming = lax.all_to_all(outgoing, ('grp', 'tile'), 0, 0, tiled=True)  33.6 us
    pallas_call x1, Pallas kernels, local(): pl.pallas_call(fold_kernel, out_shape=jax.ShapeDtypeStruct((slots, comps...  5.03 us
    all_to_all x1, other arithmetic, local(): incoming = lax.all_to_all(outgoing, ('grp', 'tile'), 0, 0, tiled=True)  1.88 us

profile of v6, /device:TPU:1, one launch (start us, length us, event | category | flops | bytes accessed | tf_op | source)
XLA Modules:
  0.0 44.6 jit_solution(13966792387615618232)
XLA Ops:
  0.0 0.9 %select_reduce_fusion = s32[256]{0:T(256)S(1)} fusion(s32[256]{0:T(256)} %bitcast.11, s32[256]{0:T(256)} %param.13), kind=kLoop, calls=%fused_computation.1 | loop fusion | flops 196352 | bytes 3072 | tf_op jit(solution)/shard_map/reduce_sum | solution.py:96
  0.9 0.1 copy.22
  1.0 0.8 %fusion.3.pick_ref = s32[256,1]{1,0:T(8,128)} fusion(s32[256,1]{1,0:T(8,128)S(1)} %copy.22, s32[]{:T(128)S(6)} %axis_index.12), kind=kLoop, calls=%fused_computation.10 | loop fusion | flops 5888 | bytes 2052 | tf_op jit(solution)/shard_map/add | solution.py:103
  1.8 5.0 %shard_map.73 = bf16[256,768]{1,0:T(8,128)(2,1)} custom-call(f32[2]{0:T(128)} %w_ref.1, bf16[129]{0:T(256)(128)(2,1)} %taps_ref.1, bf16[16,128]{1,0:T(8,128)(2,1)} %bitcast.8, bf16[16,128]{1,0:T(8,128)(2,1)} %bitcast.9, bf16[2,3,128,1024]{3,2,1,0:T(8,128)(2,1)} %bitcast.6, s32[256,1]{1,0:T(8,128)} %fusion.3.pick_ref), custom_call_target="tpu_custom_call" | custom-call | tf_op jit(solution)/shard_map/pallas_call | solution.py:104
  6.8 0.5 %broadcast.118 = bf16[]{:T(256)} broadcast(bf16[]{:T(256)} %constant.54), dimensions={} | broadcast | bytes 4 | tf_op jit(solution)/shard_map/all_to_all | solution.py:122
  7.4 1.9 %reduce.1 = bf16[256,768]{1,0:T(8,128)(2,1)S(1)} reduce(bf16[256,1,768]{2,0,1:T(8,128)(2,1)} %bitcast.7, bf16[]{:T(256)} %broadcast.118), dimensions={1}, to_apply=%copy.27.reduce_sub_computation | reduce | bytes 786434 | tf_op jit(solution)/shard_map/all_to_all | solution.py:122
  9.2 0.1 reshape.116
  9.3 33.6 %all_to_all.9 = bf16[256,2,384]{2,1,0:T(2,128)(2,1)S(1)} all-to-all(bf16[256,2,384]{2,1,0:T(2,128)(2,1)S(1)} %reshape.116), channel_id=1, replica_groups=mesh['grp'=8,'tile'=32] {'grp','tile'}, dimensions={0} | all-to-all | bytes 786432 | tf_op jit(solution)/shard_map/all_to_all | solution.py:122
  43.0 0.3 reshape.117
  43.3 0.7 %convert_reduce_fusion = f32[768]{0:T(1024)S(1)} fusion(bf16[256,1,768]{2,1,0:T(2,128)(2,1)S(1)} %reshape.117), kind=kLoop, calls=%fused_computation | loop fusion | flops 392448 | bytes 396288 | tf_op jit(solution)/shard_map/reduce_sum | solution.py:123
  44.0 0.6 %broadcast_in_dim.20 = f32[1,3,256]{2,0,1:T(1,128)} reshape(f32[768]{0:T(1024)S(1)} %convert_reduce_fusion) | data formatting | bytes 6144 | tf_op jit(solution)/shard_map/broadcast_in_dim | solution.py:126

commit v7 on v5

--- a/solution.py
+++ b/solution.py
@@ -13,10 +13,10 @@
     ctrl, tile = cols_ref.shape
     col_tiles = cols // tile
     period = taps_row.shape[1]
-    half = (taps_ref.shape[1] - 1) // 2
+    half = (taps_ref.shape[0] - 1) // 2
 
     taps_row[...] = jnp.zeros(taps_row.shape, jnp.float32)
-    taps_row[:, : taps_ref.shape[1]] = taps_ref[...].astype(jnp.float32)
+    taps_row[:, : taps_ref.shape[0]] = taps_ref[...].astype(jnp.float32)[None, :]
     base = jnp.broadcast_to(taps_row[...], (tile, period))
     blocks = []
     for b in range(3):
@@ -72,7 +72,7 @@
         ],
     )(
         inst_weight,
-        filter_taps[None, :],
+        filter_taps,
         basis_cols.T,
         basis_rows.T,
         jnp.transpose(sensitivity, (0, 2, 1, 3)),

time: 43.7 us -> 42.5 us (0.973)
  local copies, waits for them, and re-layouts: 4.05 us -> 2.8 us
    broadcast_in_dim x1 -> x0, local copies, waits for them, and re-layouts: 1.25 us -> none  [local(): filter_taps[None, :]]
where the time goes in v7:
time: 42.5 us; the launch traced here: 42.3 us
  blocking collectives  33.6 us (79%)
  Pallas kernels  3.65 us (9%)
  local copies, waits for them, and re-layouts  2.8 us (7%)
  other arithmetic  1.83 us (4%)
    all_to_all x1, blocking collectives, local(): incoming = lax.all_to_all(outgoing, ('grp', 'tile'), 0, 0, tiled=True)  33.6 us
    pallas_call x1, Pallas kernels, local(): pl.pallas_call(fold_kernel, out_shape=jax.ShapeDtypeStruct((comps, 3 * ct...  3.65 us
    reshape x2, local copies, waits for them, and re-layouts, local(): parts = parts.reshape(comps, 3, ctrl_rows, col_tiles, ctrl_cols)  1.03 us
    all_to_all x1, other arithmetic, local(): incoming = lax.all_to_all(outgoing, ('grp', 'tile'), 0, 0, tiled=True)  0.92 us

profile of v7, /device:TPU:1, one launch (start us, length us, event | category | flops | bytes accessed | tf_op | source)
XLA Modules:
  0.0 42.3 jit_solution(3871346504584509232)
XLA Ops:
  0.0 0.0 copy-start.1
  0.0 0.0 copy-start
  0.0 3.6 %shard_map.73 = bf16[3,48,128]{2,1,0:T(8,128)(2,1)} custom-call(f32[2]{0:T(128)} %w_ref.1, bf16[129]{0:T(256)(128)(2,1)} %taps_ref.1, bf16[16,128]{1,0:T(8,128)(2,1)} %bitcast.14, bf16[16,128]{1,0:T(8,128)(2,1)} %bitcast.15, bf16[2,3,128,1024]{3,2,1,0:T(8,128)(2,1)} %bitcast.12), custom_call_target="tpu_custom_call" | custom-call | tf_op jit(solution)/shard_map/pallas_call | solution.py:64
  3.7 1.0 %reshape.46 = bf16[3,3,16,8,16]{4,3,2,1,0:T(8,128)(2,1)S(1)} reshape(bf16[3,48,128]{2,1,0:T(8,128)(2,1)} %shard_map.73) | data formatting | bytes 73728 | tf_op jit(solution)/shard_map/reshape | solution.py:80
  4.7 0.3 reshape.47
  5.0 0.0 copy-done.1
  5.0 0.0 copy-done
  5.0 0.2 select_reduce_fusion
  5.2 0.3 fusion
  5.5 0.5 %broadcast.74 = bf16[]{:T(256)} broadcast(bf16[]{:T(256)} %constant.46), dimensions={} | broadcast | bytes 4 | tf_op jit(solution)/shard_map/all_to_all | solution.py:94
  6.0 0.9 %reduce.1 = bf16[256,768]{1,0:T(8,128)(2,1)S(1)} reduce(bf16[256,1,768]{2,0,1:T(8,128)(2,1)S(1)} %fusion, bf16[]{:T(256)} %broadcast.74), dimensions={1}, to_apply=%copy.12.reduce_sub_computation | reduce | bytes 786434 | tf_op jit(solution)/shard_map/all_to_all | solution.py:94
  6.9 0.1 reshape.48
  7.0 33.6 %all_to_all.9 = bf16[256,2,384]{2,1,0:T(2,128)(2,1)S(1)} all-to-all(bf16[256,2,384]{2,1,0:T(2,128)(2,1)S(1)} %reshape.48), channel_id=1, replica_groups=mesh['grp'=8,'tile'=32] {'grp','tile'}, dimensions={0} | all-to-all | bytes 786432 | tf_op jit(solution)/shard_map/all_to_all | solution.py:94
  40.6 0.3 reshape.49
  41.0 0.7 %convert_reduce_fusion = f32[768]{0:T(1024)S(1)} fusion(bf16[256,1,768]{2,1,0:T(2,128)(2,1)S(1)} %reshape.49), kind=kLoop, calls=%fused_computation.2 | loop fusion | flops 392448 | bytes 396288 | tf_op jit(solution)/shard_map/reduce_sum | solution.py:95
  41.7 0.6 %broadcast_in_dim.21 = f32[1,3,256]{2,0,1:T(1,128)} reshape(f32[768]{0:T(1024)S(1)} %convert_reduce_fusion) | data formatting | bytes 6144 | tf_op jit(solution)/shard_map/broadcast_in_dim | solution.py:98
  (2 shorter events, 0.1 us)
Async XLA Ops:
  0.0 5.0 %copy-start.1 = (s32[256]{0:T(256)S(1)}, s32[256]{0:T(256)}, u32[]{:S(2)}) copy-start(s32[256]{0:T(256)} %param.13) | copy-start | bytes 3076
  0.0 5.0 %copy-start = (s32[256,1]{0,1:T(1,128)S(1)}, s32[256,1]{0,1:T(1,128)}, u32[]{:S(2)}) copy-start(s32[256,1]{0,1:T(1,128)} %param.12) | copy-start | bytes 3076

commit v8 on v7

--- a/solution.py
+++ b/solution.py
@@ -90,12 +90,14 @@
     select = (pick[:, None] == jnp.arange(3 * col_tiles, dtype=jnp.int32)[None, :]).astype(
         jnp.bfloat16
     )
-    outgoing = jnp.dot(select, parts, preferred_element_type=jnp.float32).astype(jnp.bfloat16)
+    outgoing = jnp.einsum(
+        "ms,sab->mab", select, parts.reshape(3 * col_tiles, 2, -1), preferred_element_type=jnp.float32
+    ).astype(jnp.bfloat16)
     incoming = lax.all_to_all(outgoing, ("grp", "tile"), 0, 0, tiled=True)
     total = jnp.sum(
-        incoming.astype(jnp.float32).reshape(slots, comps, ctrl_rows * ctrl_cols), axis=0
+        incoming.astype(jnp.float32).reshape(slots, 1, comps, ctrl_rows * ctrl_cols), axis=0
     )
-    return total[None]
+    return total
 
 
 def solution(mesh):

time: 42.5 us -> 40.8 us (0.960)
  other arithmetic: 1.83 us -> 0.6 us
  local copies, waits for them, and re-layouts: 2.8 us -> 2.35 us
    all_to_all x1 -> x0, other arithmetic: 0.92 us -> none  [local(): incoming = lax.all_to_all(outgoing, ('grp', 'tile'), 0, 0, tiled=True)]
    reduce_sum x0 -> x1, local copies, waits for them, and re-layouts: none -> 0.6 us  [local(): jnp.sum(incoming.astype(jnp.float32).reshape(slots, 1, comps, ctrl_rows *...]
    broadcast_in_dim x1 -> x0, local copies, waits for them, and re-layouts: 0.59 us -> none  [local(): return total[None]]
    all_to_all x1 -> x0, local copies, waits for them, and re-layouts: 0.51 us -> none  [local(): incoming = lax.all_to_all(outgoing, ('grp', 'tile'), 0, 0, tiled=True)]
where the time goes in v8:
time: 40.8 us; the launch traced here: 40.6 us
  blocking collectives  33.6 us (82%)
  Pallas kernels  3.65 us (9%)
  local copies, waits for them, and re-layouts  2.35 us (6%)
  other arithmetic  0.6 us (1%)
    all_to_all x1, blocking collectives, local(): incoming = lax.all_to_all(outgoing, ('grp', 'tile'), 0, 0, tiled=True)  33.6 us
    pallas_call x1, Pallas kernels, local(): pl.pallas_call(fold_kernel, out_shape=jax.ShapeDtypeStruct((comps, 3 * ct...  3.65 us
    reshape x2, local copies, waits for them, and re-layouts, local(): parts = parts.reshape(comps, 3, ctrl_rows, col_tiles, ctrl_cols)  1.03 us

profile of v8, /device:TPU:1, one launch (start us, length us, event | category | flops | bytes accessed | tf_op | source)
XLA Modules:
  0.0 40.6 jit_solution(6045978805448091358)
XLA Ops:
  0.0 0.0 copy-start.1
  0.0 0.0 copy-start
  0.0 3.6 %shard_map.73 = bf16[3,48,128]{2,1,0:T(8,128)(2,1)} custom-call(f32[2]{0:T(128)} %w_ref.1, bf16[129]{0:T(256)(128)(2,1)} %taps_ref.1, bf16[16,128]{1,0:T(8,128)(2,1)} %bitcast.14, bf16[16,128]{1,0:T(8,128)(2,1)} %bitcast.15, bf16[2,3,128,1024]{3,2,1,0:T(8,128)(2,1)} %bitcast.12), custom_call_target="tpu_custom_call" | custom-call | tf_op jit(solution)/shard_map/pallas_call | solution.py:64
  3.7 1.0 %reshape.41 = bf16[3,3,16,8,16]{4,3,2,1,0:T(8,128)(2,1)S(1)} reshape(bf16[3,48,128]{2,1,0:T(8,128)(2,1)} %shard_map.73) | data formatting | bytes 73728 | tf_op jit(solution)/shard_map/reshape | solution.py:80
  4.7 0.3 reshape_reshape.3
  5.0 0.0 copy-done.1
  5.0 0.0 copy-done
  5.0 0.2 select_reduce_fusion
  5.2 0.3 convolution_convert_fusion
  5.5 0.4 %copy.15 = bf16[256,2,384]{2,1,0:T(2,128)(2,1)S(1)} copy(bf16[256,2,384]{2,0,1:T(8,128)(2,1)S(1)} %convolution_convert_fusion) | data formatting | bytes 786432 | tf_op jit(solution)/shard_map/convert_element_type | solution.py:95
  5.9 33.6 %all_to_all.5 = bf16[256,2,384]{2,1,0:T(2,128)(2,1)S(1)} all-to-all(bf16[256,2,384]{2,1,0:T(2,128)(2,1)S(1)} %copy.15), channel_id=1, replica_groups=mesh['grp'=8,'tile'=32] {'grp','tile'}, dimensions={0} | all-to-all | bytes 786432 | tf_op jit(solution)/shard_map/all_to_all | solution.py:96
  39.6 0.4 %convert_reduce_fusion = f32[2,384]{1,0:T(2,128)S(1)} fusion(bf16[256,2,384]{2,1,0:T(2,128)(2,1)S(1)} %all_to_all.5), kind=kLoop, calls=%fused_computation.1 | loop fusion | flops 392448 | bytes 396288 | tf_op jit(solution)/shard_map/reduce_sum | solution.py:97
  40.0 0.6 %reduce_sum.22 = f32[1,3,256]{2,0,1:T(1,128)} reshape(f32[2,384]{1,0:T(2,128)S(1)} %convert_reduce_fusion) | data formatting | bytes 6144 | tf_op jit(solution)/shard_map/reduce_sum | solution.py:97
  (2 shorter events, 0.1 us)
Async XLA Ops:
  0.0 5.0 %copy-start.1 = (s32[256]{0:T(256)S(1)}, s32[256]{0:T(256)}, u32[]{:S(2)}) copy-start(s32[256]{0:T(256)} %param.13) | copy-start | bytes 3076
  0.0 5.0 %copy-start = (s32[256,1]{0,1:T(1,128)S(1)}, s32[256,1]{0,1:T(1,128)}, u32[]{:S(2)}) copy-start(s32[256,1]{0,1:T(1,128)} %param.12) | copy-start | bytes 3076

commit v9 on v8

v9 whole, which is shorter than its diff:
```python
import functools

import jax
import jax.numpy as jnp
from jax import lax
from jax.experimental import pallas as pl
from jax.experimental.pallas import tpu as pltpu
from jax.sharding import PartitionSpec as P


def fold_kernel(
    w_ref, taps_ref, cols_ref, rows_ref, sens_ref, out_ref, ct_ref, taps_row, hi_ref, lo_ref, rows_mat
):
    insts, _, rows, cols = sens_ref.shape
    ctrl, tile = cols_ref.shape
    col_tiles = cols // tile
    period = taps_row.shape[1]
    half = (taps_ref.shape[0] - 1) // 2

    @pl.when(pl.program_id(0) == 0)
    def _():
        taps_row[...] = jnp.zeros(taps_row.shape, jnp.float32)
        taps_row[:, : taps_ref.shape[0]] = taps_ref[...].astype(jnp.float32)[None, :]
        base = jnp.broadcast_to(taps_row[...], (tile, period))
        blocks = []
        for b in range(3):
            rolled = pltpu.roll(base, (-(tile * (b - 1) + half)) % period, 1, stride=1, stride_axis=0)
            blocks.append(rolled[:, :tile])
        toeplitz = jnp.concatenate(blocks, axis=1).astype(jnp.bfloat16)
        bases = jnp.concatenate([cols_ref[...], rows_ref[...]], axis=0)
        smoothed = jnp.dot(bases, toeplitz, preferred_element_type=jnp.float32)
        ct_ref[...] = jnp.zeros(ct_ref.shape, jnp.float32)
        for y in range(col_tiles):
            for cb in range(max(0, y - 1), min(col_tiles, y + 2)):
                b = cb - y + 1
                ct_ref[ctrl * y : ctrl * (y + 1), tile * cb : tile * (cb + 1)] = smoothed[
                    :ctrl, tile * b : tile * (b + 1)
                ]
        ct = ct_ref[...]
        ct_hi = ct.astype(jnp.bfloat16)
        hi_ref[...] = ct_hi
        lo_ref[...] = (ct - ct_hi.astype(jnp.float32)).astype(jnp.bfloat16)
        rows_mat[...] = jnp.concatenate(
            [smoothed[ctrl:, tile * (2 - d) : tile * (3 - d)] for d in range(3)], axis=0
        )

    nt = (((1,), (1,)), ((), ()))
    summed = (sens_ref[0, 0].astype(jnp.float32) * w_ref[0]).astype(jnp.float32)
    for i in range(1, insts):
        summed = summed + sens_ref[i, 0].astype(jnp.float32) * w_ref[i]
    summed = summed.astype(jnp.bfloat16)
    by_cols = lax.dot_general(summed, hi_ref[...], nt, preferred_element_type=jnp.float32)
    by_cols = by_cols + lax.dot_general(summed, lo_ref[...], nt, preferred_element_type=jnp.float32)
    out_ref[0] = jnp.dot(
        rows_mat[...], by_cols, precision=lax.Precision.HIGHEST, preferred_element_type=jnp.float32
    ).astype(out_ref.dtype)


def local(sensitivity, inst_weight, filter_taps, basis_rows, basis_cols, box_table, owner_perm):
    tile_rows, ctrl_rows = basis_rows.shape
    tile_cols, ctrl_cols = basis_cols.shape
    insts, local_rows, comps, cols_all = sensitivity.shape
    col_tiles = cols_all // tile_cols
    slots = owner_perm.shape[0]
    assert local_rows == tile_rows and tile_rows == tile_cols and ctrl_rows == ctrl_cols

    period = 4 * tile_rows
    parts = pl.pallas_call(
        fold_kernel,
        out_shape=jax.ShapeDtypeStruct((comps, 3 * ctrl_rows, col_tiles * ctrl_cols), jnp.bfloat16),
        grid=(comps,),
        in_specs=[
            pl.BlockSpec(memory_space=pltpu.SMEM),
            pl.BlockSpec(filter_taps.shape, lambda k: (0,)),
            pl.BlockSpec(basis_cols.T.shape, lambda k: (0, 0)),
            pl.BlockSpec(basis_rows.T.shape, lambda k: (0, 0)),
            pl.BlockSpec((insts, 1, local_rows, cols_all), lambda k: (0, k, 0, 0)),
        ],
        out_specs=pl.BlockSpec((1, 3 * ctrl_rows, col_tiles * ctrl_cols), lambda k: (k, 0, 0)),
        scratch_shapes=[
            pltpu.VMEM((col_tiles * ctrl_cols, cols_all), jnp.float32),
            pltpu.VMEM((1, period), jnp.float32),
            pltpu.VMEM((col_tiles * ctrl_cols, cols_all), jnp.bfloat16),
            pltpu.VMEM((col_tiles * ctrl_cols, cols_all), jnp.bfloat16),
            pltpu.VMEM((3 * ctrl_rows, local_rows), jnp.float32),
        ],
        compiler_params=pltpu.CompilerParams(dimension_semantics=("arbitrary",)),
    )(
        inst_weight,
        filter_taps,
        basis_cols.T,
        basis_rows.T,
        jnp.transpose(sensitivity, (0, 2, 1, 3)),
    )
    parts = parts.reshape(comps, 3, ctrl_rows, col_tiles, ctrl_cols)
    parts = parts.transpose(1, 3, 0, 2, 4).reshape(3 * col_tiles, comps * ctrl_rows * ctrl_cols)

    tiles = jnp.arange(box_table.shape[0], dtype=jnp.int32)
    tile_of_slot = jnp.sum(
        jnp.where(box_table[:, 0][None, :] == owner_perm[:, None], tiles[None, :], 0), axis=1
    )
    here = lax.axis_index("tile")
    rel_row = tile_of_slot // col_tiles - here + 1
    pick = rel_row * col_tiles + tile_of_slot % col_tiles
    select = (pick[:, None] == jnp.arange(3 * col_tiles, dtype=jnp.int32)[None, :]).astype(
        jnp.bfloat16
    )
    outgoing = jnp.einsum(
        "ms,sab->mab", select, parts.reshape(3 * col_tiles, 2, -1), preferred_element_type=jnp.float32
    ).astype(jnp.bfloat16)
    incoming = lax.all_to_all(outgoing, ("grp", "tile"), 0, 0, tiled=True)
    total = jnp.sum(
        incoming.astype(jnp.float32).reshape(slots, 1, comps, ctrl_rows * ctrl_cols), axis=0
    )
    return total


def solution(mesh):
    placed = (P("grp", "tile", None, None), P("grp"), P(), P(), P(), P(), P())
    return jax.shard_map(
        local, mesh=mesh, in_specs=placed, out_specs=P(("grp", "tile"), None, None), check_vma=False
    )
```

time: 40.8 us -> 41.2 us (level)
  Pallas kernels: 3.65 us -> 4.1 us
    pallas_call x1, Pallas kernels: 3.65 us -> 4.1 us  [local(): pl.pallas_call(fold_kernel, out_shape=jax.ShapeDtypeStruct((comps, 3 * ct...]
where the time goes in v9:
time: 41.2 us; the launch traced here: 41 us
  blocking collectives  33.6 us (82%)
  Pallas kernels  4.1 us (10%)
  local copies, waits for them, and re-layouts  2.35 us (6%)
  other arithmetic  0.6 us (1%)
    all_to_all x1, blocking collectives, local(): incoming = lax.all_to_all(outgoing, ('grp', 'tile'), 0, 0, tiled=True)  33.6 us
    pallas_call x1, Pallas kernels, local(): pl.pallas_call(fold_kernel, out_shape=jax.ShapeDtypeStruct((comps, 3 * ct...  4.1 us
    reshape x2, local copies, waits for them, and re-layouts, local(): parts = parts.reshape(comps, 3, ctrl_rows, col_tiles, ctrl_cols)  1.03 us

profile of v9, /device:TPU:1, one launch (start us, length us, event | category | flops | bytes accessed | tf_op | source)
XLA Modules:
  0.0 41.0 jit_solution(5295080857927735904)
XLA Ops:
  0.0 0.0 copy-start.1
  0.0 0.0 copy-start
  0.0 4.1 %shard_map.73 = bf16[3,48,128]{2,1,0:T(8,128)(2,1)} custom-call(f32[2]{0:T(128)} %w_ref.1, bf16[129]{0:T(256)(128)(2,1)} %taps_ref.1, bf16[16,128]{1,0:T(8,128)(2,1)} %bitcast.14, bf16[16,128]{1,0:T(8,128)(2,1)} %bitcast.15, bf16[2,3,128,1024]{3,2,1,0:T(8,128)(2,1)} %bitcast.12), custom_call_target="tpu_custom_call" | custom-call | tf_op jit(solution)/shard_map/pallas_call | solution.py:68
  4.1 1.0 %reshape.41 = bf16[3,3,16,8,16]{4,3,2,1,0:T(8,128)(2,1)S(1)} reshape(bf16[3,48,128]{2,1,0:T(8,128)(2,1)} %shard_map.73) | data formatting | bytes 73728 | tf_op jit(solution)/shard_map/reshape | solution.py:95
  5.1 0.3 reshape_reshape.3
  5.5 0.0 copy-done.1
  5.5 0.0 copy-done
  5.5 0.2 select_reduce_fusion
  5.7 0.3 convolution_convert_fusion
  6.0 0.4 copy.15
  6.4 33.6 %all_to_all.5 = bf16[256,2,384]{2,1,0:T(2,128)(2,1)S(1)} all-to-all(bf16[256,2,384]{2,1,0:T(2,128)(2,1)S(1)} %copy.15), channel_id=1, replica_groups=mesh['grp'=8,'tile'=32] {'grp','tile'}, dimensions={0} | all-to-all | bytes 786432 | tf_op jit(solution)/shard_map/all_to_all | solution.py:111
  40.0 0.4 convert_reduce_fusion
  40.4 0.6 %reduce_sum.22 = f32[1,3,256]{2,0,1:T(1,128)} reshape(f32[2,384]{1,0:T(2,128)S(1)} %convert_reduce_fusion) | data formatting | bytes 6144 | tf_op jit(solution)/shard_map/reduce_sum | solution.py:112
  (2 shorter events, 0.1 us)
Async XLA Ops:
  0.0 5.5 %copy-start.1 = (s32[256]{0:T(256)S(1)}, s32[256]{0:T(256)}, u32[]{:S(2)}) copy-start(s32[256]{0:T(256)} %param.13) | copy-start | bytes 3076
  0.0 5.5 %copy-start = (s32[256,1]{0,1:T(1,128)S(1)}, s32[256,1]{0,1:T(1,128)}, u32[]{:S(2)}) copy-start(s32[256,1]{0,1:T(1,128)} %param.12) | copy-start | bytes 3076

commit v10 on v8

--- a/solution.py
+++ b/solution.py
@@ -33,9 +33,7 @@
             ct_ref[ctrl * y : ctrl * (y + 1), tile * cb : tile * (cb + 1)] = smoothed[
                 :ctrl, tile * b : tile * (b + 1)
             ]
-    ct = ct_ref[...]
-    ct_hi = ct.astype(jnp.bfloat16)
-    ct_lo = (ct - ct_hi.astype(jnp.float32)).astype(jnp.bfloat16)
+    ct = ct_ref[...].astype(jnp.bfloat16)
     rows_matrix = jnp.concatenate(
         [smoothed[ctrl:, tile * (2 - d) : tile * (3 - d)] for d in range(3)], axis=0
     )
@@ -45,8 +43,7 @@
         for i in range(1, insts):
             summed = summed + sens_ref[i, k].astype(jnp.float32) * w_ref[i]
         summed = summed.astype(jnp.bfloat16)
-        by_cols = lax.dot_general(summed, ct_hi, nt, preferred_element_type=jnp.float32)
-        by_cols = by_cols + lax.dot_general(summed, ct_lo, nt, preferred_element_type=jnp.float32)
+        by_cols = lax.dot_general(summed, ct, nt, preferred_element_type=jnp.float32)
         out_ref[k] = jnp.dot(
             rows_matrix, by_cols, precision=lax.Precision.HIGHEST, preferred_element_type=jnp.float32
         ).astype(out_ref.dtype)

time: 40.8 us -> 40.6 us (level)
  no operation moved by 1% of the time
where the time goes in v10:
time: 40.6 us; the launch traced here: 40.4 us
  blocking collectives  33.6 us (83%)
  Pallas kernels  3.52 us (9%)
  local copies, waits for them, and re-layouts  2.35 us (6%)
  other arithmetic  0.6 us (1%)
    all_to_all x1, blocking collectives, local(): incoming = lax.all_to_all(outgoing, ('grp', 'tile'), 0, 0, tiled=True)  33.6 us
    pallas_call x1, Pallas kernels, local(): pl.pallas_call(fold_kernel, out_shape=jax.ShapeDtypeStruct((comps, 3 * ct...  3.52 us
    reshape x2, local copies, waits for them, and re-layouts, local(): parts = parts.reshape(comps, 3, ctrl_rows, col_tiles, ctrl_cols)  1.03 us

profile of v10, /device:TPU:1, one launch (start us, length us, event | category | flops | bytes accessed | tf_op | source)
XLA Modules:
  0.0 40.4 jit_solution(6717265020019630294)
XLA Ops:
  0.0 0.0 copy-start.1
  0.0 0.0 copy-start
  0.0 3.5 %shard_map.73 = bf16[3,48,128]{2,1,0:T(8,128)(2,1)} custom-call(f32[2]{0:T(128)} %w_ref.1, bf16[129]{0:T(256)(128)(2,1)} %taps_ref.1, bf16[16,128]{1,0:T(8,128)(2,1)} %bitcast.14, bf16[16,128]{1,0:T(8,128)(2,1)} %bitcast.15, bf16[2,3,128,1024]{3,2,1,0:T(8,128)(2,1)} %bitcast.12), custom_call_target="tpu_custom_call" | custom-call | tf_op jit(solution)/shard_map/pallas_call | solution.py:61
  3.5 1.0 %reshape.41 = bf16[3,3,16,8,16]{4,3,2,1,0:T(8,128)(2,1)S(1)} reshape(bf16[3,48,128]{2,1,0:T(8,128)(2,1)} %shard_map.73) | data formatting | bytes 73728 | tf_op jit(solution)/shard_map/reshape | solution.py:77
  4.6 0.3 reshape_reshape.3
  4.9 0.0 copy-done.1
  4.9 0.0 copy-done
  4.9 0.2 select_reduce_fusion
  5.1 0.3 convolution_convert_fusion
  5.4 0.4 %copy.15 = bf16[256,2,384]{2,1,0:T(2,128)(2,1)S(1)} copy(bf16[256,2,384]{2,0,1:T(8,128)(2,1)S(1)} %convolution_convert_fusion) | data formatting | bytes 786432 | tf_op jit(solution)/shard_map/convert_element_type | solution.py:92
  5.8 33.6 %all_to_all.5 = bf16[256,2,384]{2,1,0:T(2,128)(2,1)S(1)} all-to-all(bf16[256,2,384]{2,1,0:T(2,128)(2,1)S(1)} %copy.15), channel_id=1, replica_groups=mesh['grp'=8,'tile'=32] {'grp','tile'}, dimensions={0} | all-to-all | bytes 786432 | tf_op jit(solution)/shard_map/all_to_all | solution.py:93
  39.4 0.4 %convert_reduce_fusion = f32[2,384]{1,0:T(2,128)S(1)} fusion(bf16[256,2,384]{2,1,0:T(2,128)(2,1)S(1)} %all_to_all.5), kind=kLoop, calls=%fused_computation.1 | loop fusion | flops 392448 | bytes 396288 | tf_op jit(solution)/shard_map/reduce_sum | solution.py:94
  39.8 0.6 %reduce_sum.22 = f32[1,3,256]{2,0,1:T(1,128)} reshape(f32[2,384]{1,0:T(2,128)S(1)} %convert_reduce_fusion) | data formatting | bytes 6144 | tf_op jit(solution)/shard_map/reduce_sum | solution.py:94
  (2 shorter events, 0.1 us)
Async XLA Ops:
  0.0 4.9 %copy-start.1 = (s32[256]{0:T(256)S(1)}, s32[256]{0:T(256)}, u32[]{:S(2)}) copy-start(s32[256]{0:T(256)} %param.13) | copy-start | bytes 3076
  0.0 4.9 %copy-start = (s32[256,1]{0,1:T(1,128)S(1)}, s32[256,1]{0,1:T(1,128)}, u32[]{:S(2)}) copy-start(s32[256,1]{0,1:T(1,128)} %param.12) | copy-start | bytes 3076

commit v11 on v8

--- a/solution.py
+++ b/solution.py
@@ -41,12 +41,13 @@
     )
     nt = (((1,), (1,)), ((), ()))
     for k in range(comps):
-        summed = (sens_ref[0, k].astype(jnp.float32) * w_ref[0]).astype(jnp.float32)
-        for i in range(1, insts):
-            summed = summed + sens_ref[i, k].astype(jnp.float32) * w_ref[i]
-        summed = summed.astype(jnp.bfloat16)
-        by_cols = lax.dot_general(summed, ct_hi, nt, preferred_element_type=jnp.float32)
-        by_cols = by_cols + lax.dot_general(summed, ct_lo, nt, preferred_element_type=jnp.float32)
+        by_cols = None
+        for i in range(insts):
+            lines = sens_ref[i, k]
+            term = lax.dot_general(lines, ct_hi, nt, preferred_element_type=jnp.float32)
+            term = term + lax.dot_general(lines, ct_lo, nt, preferred_element_type=jnp.float32)
+            term = term * w_ref[i]
+            by_cols = term if by_cols is None else by_cols + term
         out_ref[k] = jnp.dot(
             rows_matrix, by_cols, precision=lax.Precision.HIGHEST, preferred_element_type=jnp.float32
         ).astype(out_ref.dtype)

time: 40.8 us -> 41.1 us (level)
  no operation moved by 1% of the time
where the time goes in v11:
time: 41.1 us; the launch traced here: 40.9 us
  blocking collectives  33.6 us (82%)
  Pallas kernels  4.02 us (10%)
  local copies, waits for them, and re-layouts  2.35 us (6%)
  other arithmetic  0.6 us (1%)
    all_to_all x1, blocking collectives, local(): incoming = lax.all_to_all(outgoing, ('grp', 'tile'), 0, 0, tiled=True)  33.6 us
    pallas_call x1, Pallas kernels, local(): pl.pallas_call(fold_kernel, out_shape=jax.ShapeDtypeStruct((comps, 3 * ct...  4.02 us
    reshape x2, local copies, waits for them, and re-layouts, local(): parts = parts.reshape(comps, 3, ctrl_rows, col_tiles, ctrl_cols)  1.03 us

profile of v11, /device:TPU:1, one launch (start us, length us, event | category | flops | bytes accessed | tf_op | source)
XLA Modules:
  0.0 40.9 jit_solution(13242459018111515631)
XLA Ops:
  0.0 0.0 copy-start.1
  0.0 0.0 copy-start
  0.0 4.0 %shard_map.73 = bf16[3,48,128]{2,1,0:T(8,128)(2,1)} custom-call(f32[2]{0:T(128)} %w_ref.1, bf16[129]{0:T(256)(128)(2,1)} %taps_ref.1, bf16[16,128]{1,0:T(8,128)(2,1)} %bitcast.14, bf16[16,128]{1,0:T(8,128)(2,1)} %bitcast.15, bf16[2,3,128,1024]{3,2,1,0:T(8,128)(2,1)} %bitcast.12), custom_call_target="tpu_custom_call" | custom-call | tf_op jit(solution)/shard_map/pallas_call | solution.py:65
  4.0 1.0 %reshape.41 = bf16[3,3,16,8,16]{4,3,2,1,0:T(8,128)(2,1)S(1)} reshape(bf16[3,48,128]{2,1,0:T(8,128)(2,1)} %shard_map.73) | data formatting | bytes 73728 | tf_op jit(solution)/shard_map/reshape | solution.py:81
  5.1 0.3 reshape_reshape.3
  5.4 0.0 copy-done.1
  5.4 0.0 copy-done
  5.4 0.2 select_reduce_fusion
  5.6 0.3 convolution_convert_fusion
  5.9 0.4 copy.15
  6.3 33.6 %all_to_all.5 = bf16[256,2,384]{2,1,0:T(2,128)(2,1)S(1)} all-to-all(bf16[256,2,384]{2,1,0:T(2,128)(2,1)S(1)} %copy.15), channel_id=1, replica_groups=mesh['grp'=8,'tile'=32] {'grp','tile'}, dimensions={0} | all-to-all | bytes 786432 | tf_op jit(solution)/shard_map/all_to_all | solution.py:97
  39.9 0.4 convert_reduce_fusion
  40.3 0.6 %reduce_sum.22 = f32[1,3,256]{2,0,1:T(1,128)} reshape(f32[2,384]{1,0:T(2,128)S(1)} %convert_reduce_fusion) | data formatting | bytes 6144 | tf_op jit(solution)/shard_map/reduce_sum | solution.py:98
  (2 shorter events, 0.1 us)
Async XLA Ops:
  0.0 5.4 %copy-start.1 = (s32[256]{0:T(256)S(1)}, s32[256]{0:T(256)}, u32[]{:S(2)}) copy-start(s32[256]{0:T(256)} %param.13) | copy-start | bytes 3076
  0.0 5.4 %copy-start = (s32[256,1]{0,1:T(1,128)S(1)}, s32[256,1]{0,1:T(1,128)}, u32[]{:S(2)}) copy-start(s32[256,1]{0,1:T(1,128)} %param.12) | copy-start | bytes 3076

commit v12 on v6

--- a/solution.py
+++ b/solution.py
@@ -42,20 +42,6 @@
         [smoothed[ctrl:, tile * (2 - d) : tile * (3 - d)] for d in range(3)], axis=0
     )
     nt = (((1,), (1,)), ((), ()))
-    lanes = col_tiles * ctrl
-    block = ctrl * ctrl
-    spread = (
-        lax.broadcasted_iota(jnp.int32, (3 * ctrl, 3 * block), 0)
-        == lax.broadcasted_iota(jnp.int32, (3 * ctrl, 3 * block), 1) // ctrl
-    ).astype(jnp.bfloat16)
-    keep = (
-        lax.broadcasted_iota(jnp.int32, (lanes, 3 * block), 0) % ctrl
-        == lax.broadcasted_iota(jnp.int32, (lanes, 3 * block), 1) % ctrl
-    )
-    gather_y = (
-        lax.broadcasted_iota(jnp.int32, (col_tiles, lanes), 0)
-        == lax.broadcasted_iota(jnp.int32, (col_tiles, lanes), 1) // ctrl
-    ).astype(jnp.bfloat16)
     for k in range(comps):
         summed = (sens_ref[0, k].astype(jnp.float32) * w_ref[0]).astype(jnp.float32)
         for i in range(1, insts):
@@ -65,22 +51,20 @@
         by_cols = by_cols + lax.dot_general(summed, ct_lo, nt, preferred_element_type=jnp.float32)
         z = jnp.dot(
             rows_matrix, by_cols, precision=lax.Precision.HIGHEST, preferred_element_type=jnp.float32
+        ).astype(jnp.bfloat16)
+        block = ctrl * ctrl
+        parts_ref[:, block * k : block * (k + 1)] = pltpu.einshape(
+            "(dp)(yq)->(dy)(pq)", z, d=3, p=ctrl, y=col_tiles, q=ctrl
         )
-        zt = z.T.astype(jnp.bfloat16)
-        wide = jnp.dot(zt, spread, preferred_element_type=jnp.float32)
-        wide = jnp.where(keep, wide, 0.0).astype(jnp.bfloat16)
-        moved = jnp.dot(gather_y, wide, preferred_element_type=jnp.float32).astype(jnp.bfloat16)
-        for d in range(3):
-            parts_ref[col_tiles * d : col_tiles * (d + 1), block * k : block * (k + 1)] = moved[
-                :, block * d : block * (d + 1)
-            ]
-    rows_of_parts = parts_ref.shape[0]
     select = (
-        pick_ref[...] == lax.broadcasted_iota(jnp.int32, (out_ref.shape[0], rows_of_parts), 1)
+        pick_ref[...] == lax.broadcasted_iota(jnp.int32, (out_ref.shape[0], parts_ref.shape[0]), 1)
     ).astype(jnp.bfloat16)
-    out_ref[...] = jnp.dot(select, parts_ref[...], preferred_element_type=jnp.float32).astype(
+    chosen = jnp.dot(select, parts_ref[...], preferred_element_type=jnp.float32).astype(
         out_ref.dtype
     )
+    half_row = out_ref.shape[2]
+    out_ref[:, 0, :] = chosen[:, :half_row]
+    out_ref[:, 1, :] = chosen[:, half_row:]
 
 
 def local(sensitivity, inst_weight, filter_taps, basis_rows, basis_cols, box_table, owner_perm):
@@ -101,15 +85,16 @@
     here = lax.axis_index("tile")
     rel_row = tile_of_slot // col_tiles - here + 1
     pick = rel_row * col_tiles + tile_of_slot % col_tiles
+    values = comps * ctrl_rows * ctrl_cols
     outgoing = pl.pallas_call(
         fold_kernel,
-        out_shape=jax.ShapeDtypeStruct((slots, comps * ctrl_rows * ctrl_cols), jnp.bfloat16),
+        out_shape=jax.ShapeDtypeStruct((slots, 2, values // 2), jnp.bfloat16),
         in_specs=[pl.BlockSpec(memory_space=pltpu.SMEM)] + [pl.BlockSpec(memory_space=pltpu.VMEM)] * 5,
         out_specs=pl.BlockSpec(memory_space=pltpu.VMEM),
         scratch_shapes=[
             pltpu.VMEM((col_tiles * ctrl_cols, cols_all), jnp.float32),
             pltpu.VMEM((1, period), jnp.float32),
-            pltpu.VMEM((3 * col_tiles, comps * ctrl_rows * ctrl_cols), jnp.bfloat16),
+            pltpu.VMEM((3 * col_tiles, values), jnp.bfloat16),
         ],
     )(
         inst_weight,
@@ -121,13 +106,19 @@
     )
     incoming = lax.all_to_all(outgoing, ("grp", "tile"), 0, 0, tiled=True)
     total = jnp.sum(
-        incoming.astype(jnp.float32).reshape(slots, comps, ctrl_rows * ctrl_cols), axis=0
+        incoming.astype(jnp.float32).reshape(slots, 1, comps, ctrl_rows * ctrl_cols), axis=0
     )
-    return total[None]
+    return total
 
 
 def solution(mesh):
     placed = (P("grp", "tile", None, None), P("grp"), P(), P(), P(), P(), P())
-    return jax.shard_map(
+    mapped = jax.shard_map(
         local, mesh=mesh, in_specs=placed, out_specs=P(("grp", "tile"), None, None), check_vma=False
     )
+
+    def run(*args):
+        with jax.sharding.use_abstract_mesh(mesh.abstract_mesh):
+            return mapped(*args)
+
+    return run

time: 44.8 us -> 41.2 us (0.920)
  other arithmetic: 4.26 us -> 2.07 us
  local copies, waits for them, and re-layouts: 1.65 us -> 0.74 us
  Pallas kernels: 5.03 us -> 4.39 us
    all_to_all x1 -> x0, other arithmetic: 1.88 us -> none  [local(): incoming = lax.all_to_all(outgoing, ('grp', 'tile'), 0, 0, tiled=True)]
    pallas_call x1, Pallas kernels: 5.03 us -> 4.39 us  [local(): pl.pallas_call(fold_kernel, out_shape=jax.ShapeDtypeStruct((slots, 2, val...]
    reduce_sum x0 -> x1, local copies, waits for them, and re-layouts: none -> 0.6 us  [local(): jnp.sum(incoming.astype(jnp.float32).reshape(slots, 1, comps, ctrl_rows *...]
    broadcast_in_dim x1 -> x0, local copies, waits for them, and re-layouts: 0.59 us -> none  [local(): return total[None]]
    all_to_all x1 -> x0, local copies, waits for them, and re-layouts: 0.51 us -> none  [local(): incoming = lax.all_to_all(outgoing, ('grp', 'tile'), 0, 0, tiled=True)]
where the time goes in v12:
time: 41.2 us; the launch traced here: 41 us
  blocking collectives  33.8 us (82%)
  Pallas kernels  4.39 us (11%)
  other arithmetic  2.07 us (5%)
  local copies, waits for them, and re-layouts  0.74 us (2%)
    all_to_all x1, blocking collectives, local(): incoming = lax.all_to_all(outgoing, ('grp', 'tile'), 0, 0, tiled=True)  33.8 us
    pallas_call x1, Pallas kernels, local(): pl.pallas_call(fold_kernel, out_shape=jax.ShapeDtypeStruct((slots, 2, val...  4.39 us
    reduce_sum x1, other arithmetic, local(): jnp.sum(jnp.where(box_table[:, 0][None, :] == owner_perm[:, None], tiles[...  0.87 us

profile of v12, /device:TPU:1, one launch (start us, length us, event | category | flops | bytes accessed | tf_op | source)
XLA Modules:
  0.0 41.0 jit_solution(3564883354302063550)
XLA Ops:
  0.0 0.9 %select_reduce_fusion = s32[256]{0:T(256)S(1)} fusion(s32[256]{0:T(256)} %bitcast.9, s32[256]{0:T(256)} %param.13), kind=kLoop, calls=%fused_computation.1 | loop fusion | flops 196352 | bytes 3072 | tf_op jit(solution)/shard_map/reduce_sum | solution.py:80
  0.9 0.1 copy.16
  1.0 0.8 %fusion.3.pick_ref = s32[256,1]{1,0:T(8,128)} fusion(s32[256,1]{1,0:T(8,128)S(1)} %copy.16, s32[]{:T(128)S(6)} %axis_index.12), kind=kLoop, calls=%fused_computation.10 | loop fusion | flops 5888 | bytes 2052 | tf_op jit(solution)/shard_map/add | solution.py:87
  1.8 4.4 %shard_map.73 = bf16[256,2,384]{2,1,0:T(2,128)(2,1)} custom-call(f32[2]{0:T(128)} %w_ref.1, bf16[129]{0:T(256)(128)(2,1)} %taps_ref.1, bf16[16,128]{1,0:T(8,128)(2,1)} %bitcast.6, bf16[16,128]{1,0:T(8,128)(2,1)} %bitcast.7, bf16[2,3,128,1024]{3,2,1,0:T(8,128)(2,1)} %bitcast.5, s32[256,1]{1,0:T(8,128)} %fusion.3.pick_ref), custom_call_target="tpu_custom_call" | custom-call | tf_op jit(solution)/shard_map/pallas_call | solution.py:89
  6.2 33.8 %all_to_all.5 = bf16[256,2,384]{2,1,0:T(2,128)(2,1)S(1)} all-to-all(bf16[256,2,384]{2,1,0:T(2,128)(2,1)} %shard_map.73), channel_id=1, replica_groups=mesh['grp'=8,'tile'=32] {'grp','tile'}, dimensions={0} | all-to-all | bytes 786432 | tf_op jit(solution)/shard_map/all_to_all | solution.py:107
  40.0 0.4 convert_reduce_fusion
  40.4 0.6 %reduce_sum.25 = f32[1,3,256]{2,0,1:T(1,128)} reshape(f32[2,384]{1,0:T(2,128)S(1)} %convert_reduce_fusion) | data formatting | bytes 6144 | tf_op jit(solution)/shard_map/reduce_sum | solution.py:108

commit v13 on v12

--- a/solution.py
+++ b/solution.py
@@ -9,7 +9,7 @@
 
 
 def fold_kernel(
-    w_ref, taps_ref, cols_ref, rows_ref, sens_ref, pick_ref, out_ref, ct_ref, taps_row, parts_ref
+    w_ref, taps_ref, cols_ref, rows_ref, sens_ref, box_ref, owner_ref, out_ref, ct_ref, taps_row, parts_ref
 ):
     insts, comps, rows, cols = sens_ref.shape
     ctrl, tile = cols_ref.shape
@@ -56,9 +56,17 @@
         parts_ref[:, block * k : block * (k + 1)] = pltpu.einshape(
             "(dp)(yq)->(dy)(pq)", z, d=3, p=ctrl, y=col_tiles, q=ctrl
         )
-    select = (
-        pick_ref[...] == lax.broadcasted_iota(jnp.int32, (out_ref.shape[0], parts_ref.shape[0]), 1)
+    slots = owner_ref.shape[0]
+    ntiles = box_ref.shape[0]
+    owner_col = jnp.broadcast_to(owner_ref[...][None, :], (8, slots)).T[:, :1]
+    slot_tile = (owner_col == box_ref[...][None, :]).astype(jnp.bfloat16)
+    here = lax.axis_index("tile")
+    rows_of_parts = parts_ref.shape[0]
+    tile_part = (
+        lax.broadcasted_iota(jnp.int32, (ntiles, rows_of_parts), 0)
+        == lax.broadcasted_iota(jnp.int32, (ntiles, rows_of_parts), 1) + col_tiles * (here - 1)
     ).astype(jnp.bfloat16)
+    select = jnp.dot(slot_tile, tile_part, preferred_element_type=jnp.float32).astype(jnp.bfloat16)
     chosen = jnp.dot(select, parts_ref[...], preferred_element_type=jnp.float32).astype(
         out_ref.dtype
     )
@@ -76,20 +84,11 @@
     assert local_rows == tile_rows and tile_rows == tile_cols and ctrl_rows == ctrl_cols
 
     period = 4 * tile_rows
-    tiles = jnp.arange(box_table.shape[0], dtype=jnp.int32)
-    tile_of_slot = jnp.sum(
-        jnp.where(box_table[:, 0][None, :] == owner_perm[:, None], tiles[None, :], 0),
-        axis=1,
-        keepdims=True,
-    )
-    here = lax.axis_index("tile")
-    rel_row = tile_of_slot // col_tiles - here + 1
-    pick = rel_row * col_tiles + tile_of_slot % col_tiles
     values = comps * ctrl_rows * ctrl_cols
     outgoing = pl.pallas_call(
         fold_kernel,
         out_shape=jax.ShapeDtypeStruct((slots, 2, values // 2), jnp.bfloat16),
-        in_specs=[pl.BlockSpec(memory_space=pltpu.SMEM)] + [pl.BlockSpec(memory_space=pltpu.VMEM)] * 5,
+        in_specs=[pl.BlockSpec(memory_space=pltpu.SMEM)] + [pl.BlockSpec(memory_space=pltpu.VMEM)] * 6,
         out_specs=pl.BlockSpec(memory_space=pltpu.VMEM),
         scratch_shapes=[
             pltpu.VMEM((col_tiles * ctrl_cols, cols_all), jnp.float32),
@@ -102,7 +101,8 @@
         basis_cols.T,
         basis_rows.T,
         jnp.transpose(sensitivity, (0, 2, 1, 3)),
-        pick,
+        box_table[:, 0],
+        owner_perm,
     )
     incoming = lax.all_to_all(outgoing, ("grp", "tile"), 0, 0, tiled=True)
     total = jnp.sum(

time: 41.2 us -> 39.4 us (0.956)
  other arithmetic: 2.07 us -> 0.41 us
    reduce_sum x1 -> x0, other arithmetic: 0.87 us -> none  [local(): jnp.sum(jnp.where(box_table[:, 0][None, :] == owner_perm[:, None], tiles[...]
    add x1 -> x0, other arithmetic: 0.79 us -> none  [local(): pick = rel_row * col_tiles + tile_of_slot % col_tiles]
where the time goes in v13:
time: 39.4 us; the launch traced here: 39.2 us
  blocking collectives  33.8 us (86%)
  Pallas kernels  4.41 us (11%)
  local copies, waits for them, and re-layouts  0.6 us (2%)
  other arithmetic  0.41 us (1%)
    all_to_all x1, blocking collectives, local(): incoming = lax.all_to_all(outgoing, ('grp', 'tile'), 0, 0, tiled=True)  33.8 us
    pallas_call x1, Pallas kernels, local(): pl.pallas_call(fold_kernel, out_shape=jax.ShapeDtypeStruct((slots, 2, val...  4.41 us

profile of v13, /device:TPU:1, one launch (start us, length us, event | category | flops | bytes accessed | tf_op | source)
XLA Modules:
  0.0 39.2 jit_solution(15876489705001628530)
XLA Ops:
  0.0 4.4 %shard_map.73 = bf16[256,2,384]{2,1,0:T(2,128)(2,1)} custom-call(f32[2]{0:T(128)} %w_ref.1, bf16[129]{0:T(256)(128)(2,1)} %taps_ref.1, bf16[16,128]{1,0:T(8,128)(2,1)} %bitcast.5, bf16[16,128]{1,0:T(8,128)(2,1)} %bitcast.6, bf16[2,3,128,1024]{3,2,1,0:T(8,128)(2,1)} %bitcast.4, s32[256]{0:T(256)} %bitcast.7, s32[256]{0:T(256)} %owner_ref.1), custom_call_target="tpu_custom_call" | custom-call | tf_op jit(solution)/shard_map/pallas_call | solution.py:88
  4.4 33.8 %all_to_all.5 = bf16[256,2,384]{2,1,0:T(2,128)(2,1)S(1)} all-to-all(bf16[256,2,384]{2,1,0:T(2,128)(2,1)} %shard_map.73), channel_id=1, replica_groups=mesh['grp'=8,'tile'=32] {'grp','tile'}, dimensions={0} | all-to-all | bytes 786432 | tf_op jit(solution)/shard_map/all_to_all | solution.py:107
  38.2 0.4 %convert_reduce_fusion = f32[2,384]{1,0:T(2,128)S(1)} fusion(bf16[256,2,384]{2,1,0:T(2,128)(2,1)S(1)} %all_to_all.5), kind=kLoop, calls=%fused_computation | loop fusion | flops 392448 | bytes 396288 | tf_op jit(solution)/shard_map/reduce_sum | solution.py:108
  38.6 0.6 %reduce_sum.12 = f32[1,3,256]{2,0,1:T(1,128)} reshape(f32[2,384]{1,0:T(2,128)S(1)} %convert_reduce_fusion) | data formatting | bytes 6144 | tf_op jit(solution)/shard_map/reduce_sum | solution.py:108

commit v14 on v13

--- a/solution.py
+++ b/solution.py
@@ -75,6 +75,10 @@
     out_ref[:, 1, :] = chosen[:, half_row:]
 
 
+def sum_kernel(in_ref, out_ref):
+    out_ref[...] = jnp.sum(in_ref[...].astype(jnp.float32), axis=0)
+
+
 def local(sensitivity, inst_weight, filter_taps, basis_rows, basis_cols, box_table, owner_perm):
     tile_rows, ctrl_rows = basis_rows.shape
     tile_cols, ctrl_cols = basis_cols.shape
@@ -105,10 +109,13 @@
         owner_perm,
     )
     incoming = lax.all_to_all(outgoing, ("grp", "tile"), 0, 0, tiled=True)
-    total = jnp.sum(
-        incoming.astype(jnp.float32).reshape(slots, 1, comps, ctrl_rows * ctrl_cols), axis=0
-    )
-    return total
+    total = pl.pallas_call(
+        sum_kernel,
+        out_shape=jax.ShapeDtypeStruct(incoming.shape[1:], jnp.float32),
+        in_specs=[pl.BlockSpec(memory_space=pltpu.VMEM)],
+        out_specs=pl.BlockSpec(memory_space=pltpu.VMEM),
+    )(incoming)
+    return total.reshape(1, comps, ctrl_rows * ctrl_cols)
 
 
 def solution(mesh):

time: 39.4 us -> 41.8 us (1.061)
  Pallas kernels: 4.41 us -> 6.4 us
  local copies, waits for them, and re-layouts: 0.6 us -> 1.26 us
    pallas_call x0 -> x1, Pallas kernels: none -> 1.99 us  [local(): pl.pallas_call(sum_kernel, out_shape=jax.ShapeDtypeStruct(incoming.shape[...]
    reshape x0 -> x1, local copies, waits for them, and re-layouts: none -> 1.26 us  [local(): return total.reshape(1, comps, ctrl_rows * ctrl_cols)]
    reduce_sum x1 -> x0, local copies, waits for them, and re-layouts: 0.6 us -> none  [local(): jnp.sum(incoming.astype(jnp.float32).reshape(slots, 1, comps, ctrl_rows *...]
where the time goes in v14:
time: 41.8 us; the launch traced here: 41.6 us
  blocking collectives  33.9 us (81%)
  Pallas kernels  6.4 us (15%)
  local copies, waits for them, and re-layouts  1.26 us (3%)
    all_to_all x1, blocking collectives, local(): incoming = lax.all_to_all(outgoing, ('grp', 'tile'), 0, 0, tiled=True)  33.9 us
    pallas_call x1, Pallas kernels, local(): pl.pallas_call(fold_kernel, out_shape=jax.ShapeDtypeStruct((slots, 2, val...  4.42 us
    pallas_call x1, Pallas kernels, local(): pl.pallas_call(sum_kernel, out_shape=jax.ShapeDtypeStruct(incoming.shape[...  1.99 us
    reshape x1, local copies, waits for them, and re-layouts, local(): return total.reshape(1, comps, ctrl_rows * ctrl_cols)  1.26 us

profile of v14, /device:TPU:1, one launch (start us, length us, event | category | flops | bytes accessed | tf_op | source)
XLA Modules:
  0.0 41.6 jit_solution(4846663925013596963)
XLA Ops:
  0.0 4.4 %shard_map.73 = bf16[256,2,384]{2,1,0:T(2,128)(2,1)} custom-call(f32[2]{0:T(128)} %w_ref.1, bf16[129]{0:T(256)(128)(2,1)} %taps_ref.1, bf16[16,128]{1,0:T(8,128)(2,1)} %bitcast.5, bf16[16,128]{1,0:T(8,128)(2,1)} %bitcast.6, bf16[2,3,128,1024]{3,2,1,0:T(8,128)(2,1)} %bitcast.4, s32[256]{0:T(256)} %bitcast.7, s32[256]{0:T(256)} %owner_ref.1), custom_call_target="tpu_custom_call" | custom-call | tf_op jit(solution)/shard_map/pallas_call | solution.py:92
  4.4 33.9 %all_to_all.5.in_ref = bf16[256,2,384]{2,1,0:T(2,128)(2,1)} all-to-all(bf16[256,2,384]{2,1,0:T(2,128)(2,1)} %shard_map.73), channel_id=1, replica_groups=mesh['grp'=8,'tile'=32] {'grp','tile'}, dimensions={0} | all-to-all | bytes 786432 | tf_op jit(solution)/shard_map/all_to_all | solution.py:111
  38.3 2.0 %shard_map.74 = f32[2,384]{1,0:T(2,128)} custom-call(bf16[256,2,384]{2,1,0:T(2,128)(2,1)} %all_to_all.5.in_ref), custom_call_target="tpu_custom_call" | custom-call | tf_op jit(solution)/shard_map/pallas_call | solution.py:112
  40.3 1.3 %reshape.4 = f32[1,3,256]{2,0,1:T(1,128)} reshape(f32[2,384]{1,0:T(2,128)} %shard_map.74) | data formatting | bytes 6144 | tf_op jit(solution)/shard_map/reshape | solution.py:118

commit v15 on v13

--- a/solution.py
+++ b/solution.py
@@ -9,9 +9,26 @@
 
 
 def fold_kernel(
-    w_ref, taps_ref, cols_ref, rows_ref, sens_ref, box_ref, owner_ref, out_ref, ct_ref, taps_row, parts_ref
+    w_ref,
+    taps_ref,
+    cols_ref,
+    rows_ref,
+    sens_hbm,
+    box_ref,
+    owner_ref,
+    out_ref,
+    ct_ref,
+    taps_row,
+    parts_ref,
+    sens_ref,
+    sems,
 ):
     insts, comps, rows, cols = sens_ref.shape
+    copies = [
+        pltpu.make_async_copy(sens_hbm.at[:, k], sens_ref.at[:, k], sems.at[k]) for k in range(comps)
+    ]
+    for copy in copies:
+        copy.start()
     ctrl, tile = cols_ref.shape
     col_tiles = cols // tile
     period = taps_row.shape[1]
@@ -43,6 +60,7 @@
     )
     nt = (((1,), (1,)), ((), ()))
     for k in range(comps):
+        copies[k].wait()
         summed = (sens_ref[0, k].astype(jnp.float32) * w_ref[0]).astype(jnp.float32)
         for i in range(1, insts):
             summed = summed + sens_ref[i, k].astype(jnp.float32) * w_ref[i]
@@ -88,12 +106,17 @@
     outgoing = pl.pallas_call(
         fold_kernel,
         out_shape=jax.ShapeDtypeStruct((slots, 2, values // 2), jnp.bfloat16),
-        in_specs=[pl.BlockSpec(memory_space=pltpu.SMEM)] + [pl.BlockSpec(memory_space=pltpu.VMEM)] * 6,
+        in_specs=[pl.BlockSpec(memory_space=pltpu.SMEM)]
+        + [pl.BlockSpec(memory_space=pltpu.VMEM)] * 3
+        + [pl.BlockSpec(memory_space=pl.ANY)]
+        + [pl.BlockSpec(memory_space=pltpu.VMEM)] * 2,
         out_specs=pl.BlockSpec(memory_space=pltpu.VMEM),
         scratch_shapes=[
             pltpu.VMEM((col_tiles * ctrl_cols, cols_all), jnp.float32),
             pltpu.VMEM((1, period), jnp.float32),
             pltpu.VMEM((3 * col_tiles, values), jnp.bfloat16),
+            pltpu.VMEM((insts, comps, local_rows, cols_all), sensitivity.dtype),
+            pltpu.SemaphoreType.DMA((comps,)),
         ],
     )(
         inst_weight,

time: 39.4 us -> 40.5 us (1.028)
  Pallas kernels: 4.41 us -> 5.44 us
    pallas_call x1, Pallas kernels: 4.41 us -> 5.44 us  [local(): pl.pallas_call(fold_kernel, out_shape=jax.ShapeDtypeStruct((slots, 2, val...]
where the time goes in v15:
time: 40.5 us; the launch traced here: 40.3 us
  blocking collectives  33.8 us (83%)
  Pallas kernels  5.44 us (13%)
  local copies, waits for them, and re-layouts  0.6 us (1%)
  other arithmetic  0.41 us (1%)
    all_to_all x1, blocking collectives, local(): incoming = lax.all_to_all(outgoing, ('grp', 'tile'), 0, 0, tiled=True)  33.8 us
    pallas_call x1, Pallas kernels, local(): pl.pallas_call(fold_kernel, out_shape=jax.ShapeDtypeStruct((slots, 2, val...  5.44 us

profile of v15, /device:TPU:1, one launch (start us, length us, event | category | flops | bytes accessed | tf_op | source)
XLA Modules:
  0.0 40.3 jit_solution(4530688070852714361)
XLA Ops:
  0.0 5.4 %shard_map.73 = bf16[256,2,384]{2,1,0:T(2,128)(2,1)} custom-call(f32[2]{0:T(128)} %w_ref.1, bf16[129]{0:T(256)(128)(2,1)} %taps_ref.1, bf16[16,128]{1,0:T(8,128)(2,1)} %bitcast.5, bf16[16,128]{1,0:T(8,128)(2,1)} %bitcast.6, bf16[2,3,128,1024]{3,2,1,0:T(8,128)(2,1)} %bitcast.4, s32[256]{0:T(256)} %bitcast.7, s32[256]{0:T(256)} %owner_ref.1), custom_call_target="tpu_custom_call" | custom-call | tf_op jit(solution)/shard_map/pallas_call | solution.py:106
  5.4 33.8 %all_to_all.5 = bf16[256,2,384]{2,1,0:T(2,128)(2,1)S(1)} all-to-all(bf16[256,2,384]{2,1,0:T(2,128)(2,1)} %shard_map.73), channel_id=1, replica_groups=mesh['grp'=8,'tile'=32] {'grp','tile'}, dimensions={0} | all-to-all | bytes 786432 | tf_op jit(solution)/shard_map/all_to_all | solution.py:130
  39.3 0.4 %convert_reduce_fusion = f32[2,384]{1,0:T(2,128)S(1)} fusion(bf16[256,2,384]{2,1,0:T(2,128)(2,1)S(1)} %all_to_all.5), kind=kLoop, calls=%fused_computation | loop fusion | flops 392448 | bytes 396288 | tf_op jit(solution)/shard_map/reduce_sum | solution.py:131
  39.7 0.6 %reduce_sum.12 = f32[1,3,256]{2,0,1:T(1,128)} reshape(f32[2,384]{1,0:T(2,128)S(1)} %convert_reduce_fusion) | data formatting | bytes 6144 | tf_op jit(solution)/shard_map/reduce_sum | solution.py:131

commit v16 on v13

--- a/solution.py
+++ b/solution.py
@@ -41,6 +41,8 @@
     rows_matrix = jnp.concatenate(
         [smoothed[ctrl:, tile * (2 - d) : tile * (3 - d)] for d in range(3)], axis=0
     )
+    rows_hi = rows_matrix.astype(jnp.bfloat16)
+    rows_lo = (rows_matrix - rows_hi.astype(jnp.float32)).astype(jnp.bfloat16)
     nt = (((1,), (1,)), ((), ()))
     for k in range(comps):
         summed = (sens_ref[0, k].astype(jnp.float32) * w_ref[0]).astype(jnp.float32)
@@ -49,9 +51,11 @@
         summed = summed.astype(jnp.bfloat16)
         by_cols = lax.dot_general(summed, ct_hi, nt, preferred_element_type=jnp.float32)
         by_cols = by_cols + lax.dot_general(summed, ct_lo, nt, preferred_element_type=jnp.float32)
-        z = jnp.dot(
-            rows_matrix, by_cols, precision=lax.Precision.HIGHEST, preferred_element_type=jnp.float32
-        ).astype(jnp.bfloat16)
+        cols_hi = by_cols.astype(jnp.bfloat16)
+        cols_lo = (by_cols - cols_hi.astype(jnp.float32)).astype(jnp.bfloat16)
+        z = jnp.dot(rows_hi, cols_hi, preferred_element_type=jnp.float32)
+        z = z + jnp.dot(rows_hi, cols_lo, preferred_element_type=jnp.float32)
+        z = (z + jnp.dot(rows_lo, cols_hi, preferred_element_type=jnp.float32)).astype(jnp.bfloat16)
         block = ctrl * ctrl
         parts_ref[:, block * k : block * (k + 1)] = pltpu.einshape(
             "(dp)(yq)->(dy)(pq)", z, d=3, p=ctrl, y=col_tiles, q=ctrl

time: 39.4 us -> 39.2 us (level)
  no operation moved by 1% of the time
where the time goes in v16:
time: 39.2 us; the launch traced here: 39.1 us
  blocking collectives  33.8 us (86%)
  Pallas kernels  4.24 us (11%)
  local copies, waits for them, and re-layouts  0.6 us (2%)
  other arithmetic  0.41 us (1%)
    all_to_all x1, blocking collectives, local(): incoming = lax.all_to_all(outgoing, ('grp', 'tile'), 0, 0, tiled=True)  33.8 us
    pallas_call x1, Pallas kernels, local(): pl.pallas_call(fold_kernel, out_shape=jax.ShapeDtypeStruct((slots, 2, val...  4.24 us

profile of v16, /device:TPU:1, one launch (start us, length us, event | category | flops | bytes accessed | tf_op | source)
XLA Modules:
  0.0 39.1 jit_solution(3354689089043872978)
XLA Ops:
  0.0 4.2 %shard_map.73 = bf16[256,2,384]{2,1,0:T(2,128)(2,1)} custom-call(f32[2]{0:T(128)} %w_ref.1, bf16[129]{0:T(256)(128)(2,1)} %taps_ref.1, bf16[16,128]{1,0:T(8,128)(2,1)} %bitcast.5, bf16[16,128]{1,0:T(8,128)(2,1)} %bitcast.6, bf16[2,3,128,1024]{3,2,1,0:T(8,128)(2,1)} %bitcast.4, s32[256]{0:T(256)} %bitcast.7, s32[256]{0:T(256)} %owner_ref.1), custom_call_target="tpu_custom_call" | custom-call | tf_op jit(solution)/shard_map/pallas_call | solution.py:92
  4.2 33.8 %all_to_all.5 = bf16[256,2,384]{2,1,0:T(2,128)(2,1)S(1)} all-to-all(bf16[256,2,384]{2,1,0:T(2,128)(2,1)} %shard_map.73), channel_id=1, replica_groups=mesh['grp'=8,'tile'=32] {'grp','tile'}, dimensions={0} | all-to-all | bytes 786432 | tf_op jit(solution)/shard_map/all_to_all | solution.py:111
  38.1 0.4 %convert_reduce_fusion = f32[2,384]{1,0:T(2,128)S(1)} fusion(bf16[256,2,384]{2,1,0:T(2,128)(2,1)S(1)} %all_to_all.5), kind=kLoop, calls=%fused_computation | loop fusion | flops 392448 | bytes 396288 | tf_op jit(solution)/shard_map/reduce_sum | solution.py:112
  38.5 0.6 %reduce_sum.12 = f32[1,3,256]{2,0,1:T(1,128)} reshape(f32[2,384]{1,0:T(2,128)S(1)} %convert_reduce_fusion) | data formatting | bytes 6144 | tf_op jit(solution)/shard_map/reduce_sum | solution.py:112

commit v17 on v15

--- a/solution.py
+++ b/solution.py
@@ -21,14 +21,11 @@
     taps_row,
     parts_ref,
     sens_ref,
-    sems,
+    sem,
 ):
     insts, comps, rows, cols = sens_ref.shape
-    copies = [
-        pltpu.make_async_copy(sens_hbm.at[:, k], sens_ref.at[:, k], sems.at[k]) for k in range(comps)
-    ]
-    for copy in copies:
-        copy.start()
+    arrival = pltpu.make_async_copy(sens_hbm, sens_ref, sem)
+    arrival.start()
     ctrl, tile = cols_ref.shape
     col_tiles = cols // tile
     period = taps_row.shape[1]
@@ -58,18 +55,22 @@
     rows_matrix = jnp.concatenate(
         [smoothed[ctrl:, tile * (2 - d) : tile * (3 - d)] for d in range(3)], axis=0
     )
+    rows_hi = rows_matrix.astype(jnp.bfloat16)
+    rows_lo = (rows_matrix - rows_hi.astype(jnp.float32)).astype(jnp.bfloat16)
     nt = (((1,), (1,)), ((), ()))
+    arrival.wait()
     for k in range(comps):
-        copies[k].wait()
         summed = (sens_ref[0, k].astype(jnp.float32) * w_ref[0]).astype(jnp.float32)
         for i in range(1, insts):
             summed = summed + sens_ref[i, k].astype(jnp.float32) * w_ref[i]
         summed = summed.astype(jnp.bfloat16)
         by_cols = lax.dot_general(summed, ct_hi, nt, preferred_element_type=jnp.float32)
         by_cols = by_cols + lax.dot_general(summed, ct_lo, nt, preferred_element_type=jnp.float32)
-        z = jnp.dot(
-            rows_matrix, by_cols, precision=lax.Precision.HIGHEST, preferred_element_type=jnp.float32
-        ).astype(jnp.bfloat16)
+        cols_hi = by_cols.astype(jnp.bfloat16)
+        cols_lo = (by_cols - cols_hi.astype(jnp.float32)).astype(jnp.bfloat16)
+        z = jnp.dot(rows_hi, cols_hi, preferred_element_type=jnp.float32)
+        z = z + jnp.dot(rows_hi, cols_lo, preferred_element_type=jnp.float32)
+        z = (z + jnp.dot(rows_lo, cols_hi, preferred_element_type=jnp.float32)).astype(jnp.bfloat16)
         block = ctrl * ctrl
         parts_ref[:, block * k : block * (k + 1)] = pltpu.einshape(
             "(dp)(yq)->(dy)(pq)", z, d=3, p=ctrl, y=col_tiles, q=ctrl
@@ -116,7 +117,7 @@
             pltpu.VMEM((1, period), jnp.float32),
             pltpu.VMEM((3 * col_tiles, values), jnp.bfloat16),
             pltpu.VMEM((insts, comps, local_rows, cols_all), sensitivity.dtype),
-            pltpu.SemaphoreType.DMA((comps,)),
+            pltpu.SemaphoreType.DMA(()),
         ],
     )(
         inst_weight,

time: 40.5 us -> 39.8 us (0.983)
  Pallas kernels: 5.44 us -> 4.82 us
    pallas_call x1, Pallas kernels: 5.44 us -> 4.82 us  [local(): pl.pallas_call(fold_kernel, out_shape=jax.ShapeDtypeStruct((slots, 2, val...]
where the time goes in v17:
time: 39.8 us; the launch traced here: 39.7 us
  blocking collectives  33.8 us (85%)
  Pallas kernels  4.82 us (12%)
  local copies, waits for them, and re-layouts  0.6 us (2%)
  other arithmetic  0.41 us (1%)
    all_to_all x1, blocking collectives, local(): incoming = lax.all_to_all(outgoing, ('grp', 'tile'), 0, 0, tiled=True)  33.8 us
    pallas_call x1, Pallas kernels, local(): pl.pallas_call(fold_kernel, out_shape=jax.ShapeDtypeStruct((slots, 2, val...  4.82 us

profile of v17, /device:TPU:1, one launch (start us, length us, event | category | flops | bytes accessed | tf_op | source)
XLA Modules:
  0.0 39.7 jit_solution(15582306067829289952)
XLA Ops:
  0.0 4.8 %shard_map.73 = bf16[256,2,384]{2,1,0:T(2,128)(2,1)} custom-call(f32[2]{0:T(128)} %w_ref.1, bf16[129]{0:T(256)(128)(2,1)} %taps_ref.1, bf16[16,128]{1,0:T(8,128)(2,1)} %bitcast.5, bf16[16,128]{1,0:T(8,128)(2,1)} %bitcast.6, bf16[2,3,128,1024]{3,2,1,0:T(8,128)(2,1)} %bitcast.4, s32[256]{0:T(256)} %bitcast.7, s32[256]{0:T(256)} %owner_ref.1), custom_call_target="tpu_custom_call" | custom-call | tf_op jit(solution)/shard_map/pallas_call | solution.py:107
  4.8 33.8 %all_to_all.5 = bf16[256,2,384]{2,1,0:T(2,128)(2,1)S(1)} all-to-all(bf16[256,2,384]{2,1,0:T(2,128)(2,1)} %shard_map.73), channel_id=1, replica_groups=mesh['grp'=8,'tile'=32] {'grp','tile'}, dimensions={0} | all-to-all | bytes 786432 | tf_op jit(solution)/shard_map/all_to_all | solution.py:131
  38.7 0.4 %convert_reduce_fusion = f32[2,384]{1,0:T(2,128)S(1)} fusion(bf16[256,2,384]{2,1,0:T(2,128)(2,1)S(1)} %all_to_all.5), kind=kLoop, calls=%fused_computation | loop fusion | flops 392448 | bytes 396288 | tf_op jit(solution)/shard_map/reduce_sum | solution.py:132
  39.1 0.6 %reduce_sum.12 = f32[1,3,256]{2,0,1:T(1,128)} reshape(f32[2,384]{1,0:T(2,128)S(1)} %convert_reduce_fusion) | data formatting | bytes 6144 | tf_op jit(solution)/shard_map/reduce_sum | solution.py:132

commit v18 on v16

--- a/solution.py
+++ b/solution.py
@@ -9,7 +9,7 @@
 
 
 def fold_kernel(
-    w_ref, taps_ref, cols_ref, rows_ref, sens_ref, box_ref, owner_ref, out_ref, ct_ref, taps_row, parts_ref
+    w_ref, taps_ref, cols_ref, rows_ref, sens_ref, box_ref, owner_ref, out_ref, taps_row, parts_ref
 ):
     insts, comps, rows, cols = sens_ref.shape
     ctrl, tile = cols_ref.shape
@@ -28,14 +28,22 @@
     bases = jnp.concatenate([cols_ref[...], rows_ref[...]], axis=0)
     smoothed = jnp.dot(bases, toeplitz, preferred_element_type=jnp.float32)
 
-    ct_ref[...] = jnp.zeros(ct_ref.shape, jnp.float32)
-    for y in range(col_tiles):
-        for cb in range(max(0, y - 1), min(col_tiles, y + 2)):
-            b = cb - y + 1
-            ct_ref[ctrl * y : ctrl * (y + 1), tile * cb : tile * (cb + 1)] = smoothed[
-                :ctrl, tile * b : tile * (b + 1)
-            ]
-    ct = ct_ref[...]
+    empty = jnp.zeros((ctrl, tile), jnp.float32)
+    ct = jnp.concatenate(
+        [
+            jnp.concatenate(
+                [
+                    smoothed[:ctrl, tile * (cb - y + 1) : tile * (cb - y + 2)]
+                    if abs(cb - y) <= 1
+                    else empty
+                    for cb in range(col_tiles)
+                ],
+                axis=1,
+            )
+            for y in range(col_tiles)
+        ],
+        axis=0,
+    )
     ct_hi = ct.astype(jnp.bfloat16)
     ct_lo = (ct - ct_hi.astype(jnp.float32)).astype(jnp.bfloat16)
     rows_matrix = jnp.concatenate(
@@ -95,7 +103,6 @@
         in_specs=[pl.BlockSpec(memory_space=pltpu.SMEM)] + [pl.BlockSpec(memory_space=pltpu.VMEM)] * 6,
         out_specs=pl.BlockSpec(memory_space=pltpu.VMEM),
         scratch_shapes=[
-            pltpu.VMEM((col_tiles * ctrl_cols, cols_all), jnp.float32),
             pltpu.VMEM((1, period), jnp.float32),
             pltpu.VMEM((3 * col_tiles, values), jnp.bfloat16),
         ],

time: 39.2 us -> 39.2 us (level)
  no operation moved by 1% of the time
where the time goes in v18:
time: 39.2 us; the launch traced here: 39.1 us
  blocking collectives  33.8 us (86%)
  Pallas kernels  4.24 us (11%)
  local copies, waits for them, and re-layouts  0.6 us (2%)
  other arithmetic  0.41 us (1%)
    all_to_all x1, blocking collectives, local(): incoming = lax.all_to_all(outgoing, ('grp', 'tile'), 0, 0, tiled=True)  33.8 us
    pallas_call x1, Pallas kernels, local(): pl.pallas_call(fold_kernel, out_shape=jax.ShapeDtypeStruct((slots, 2, val...  4.24 us

profile of v18, /device:TPU:1, one launch (start us, length us, event | category | flops | bytes accessed | tf_op | source)
XLA Modules:
  0.0 39.1 jit_solution(3354689089043872978)
XLA Ops:
  0.0 4.2 %shard_map.73 = bf16[256,2,384]{2,1,0:T(2,128)(2,1)} custom-call(f32[2]{0:T(128)} %w_ref.1, bf16[129]{0:T(256)(128)(2,1)} %taps_ref.1, bf16[16,128]{1,0:T(8,128)(2,1)} %bitcast.5, bf16[16,128]{1,0:T(8,128)(2,1)} %bitcast.6, bf16[2,3,128,1024]{3,2,1,0:T(8,128)(2,1)} %bitcast.4, s32[256]{0:T(256)} %bitcast.7, s32[256]{0:T(256)} %owner_ref.1), custom_call_target="tpu_custom_call" | custom-call | tf_op jit(solution)/shard_map/pallas_call | solution.py:100
  4.2 33.8 %all_to_all.5 = bf16[256,2,384]{2,1,0:T(2,128)(2,1)S(1)} all-to-all(bf16[256,2,384]{2,1,0:T(2,128)(2,1)} %shard_map.73), channel_id=1, replica_groups=mesh['grp'=8,'tile'=32] {'grp','tile'}, dimensions={0} | all-to-all | bytes 786432 | tf_op jit(solution)/shard_map/all_to_all | solution.py:118
  38.1 0.4 %convert_reduce_fusion = f32[2,384]{1,0:T(2,128)S(1)} fusion(bf16[256,2,384]{2,1,0:T(2,128)(2,1)S(1)} %all_to_all.5), kind=kLoop, calls=%fused_computation | loop fusion | flops 392448 | bytes 396288 | tf_op jit(solution)/shard_map/reduce_sum | solution.py:119
  38.5 0.6 %reduce_sum.12 = f32[1,3,256]{2,0,1:T(1,128)} reshape(f32[2,384]{1,0:T(2,128)S(1)} %convert_reduce_fusion) | data formatting | bytes 6144 | tf_op jit(solution)/shard_map/reduce_sum | solution.py:119

commit v19 on v16

--- a/solution.py
+++ b/solution.py
@@ -35,9 +35,7 @@
             ct_ref[ctrl * y : ctrl * (y + 1), tile * cb : tile * (cb + 1)] = smoothed[
                 :ctrl, tile * b : tile * (b + 1)
             ]
-    ct = ct_ref[...]
-    ct_hi = ct.astype(jnp.bfloat16)
-    ct_lo = (ct - ct_hi.astype(jnp.float32)).astype(jnp.bfloat16)
+    ct = ct_ref[...].astype(jnp.bfloat16)
     rows_matrix = jnp.concatenate(
         [smoothed[ctrl:, tile * (2 - d) : tile * (3 - d)] for d in range(3)], axis=0
     )
@@ -49,8 +47,7 @@
         for i in range(1, insts):
             summed = summed + sens_ref[i, k].astype(jnp.float32) * w_ref[i]
         summed = summed.astype(jnp.bfloat16)
-        by_cols = lax.dot_general(summed, ct_hi, nt, preferred_element_type=jnp.float32)
-        by_cols = by_cols + lax.dot_general(summed, ct_lo, nt, preferred_element_type=jnp.float32)
+        by_cols = lax.dot_general(summed, ct, nt, preferred_element_type=jnp.float32)
         cols_hi = by_cols.astype(jnp.bfloat16)
         cols_lo = (by_cols - cols_hi.astype(jnp.float32)).astype(jnp.bfloat16)
         z = jnp.dot(rows_hi, cols_hi, preferred_element_type=jnp.float32)

time: 39.2 us -> 38.9 us (level)
  no operation moved by 1% of the time
where the time goes in v19:
time: 38.9 us; the launch traced here: 38.8 us
  blocking collectives  33.8 us (87%)
  Pallas kernels  3.97 us (10%)
  local copies, waits for them, and re-layouts  0.6 us (2%)
  other arithmetic  0.41 us (1%)
    all_to_all x1, blocking collectives, local(): incoming = lax.all_to_all(outgoing, ('grp', 'tile'), 0, 0, tiled=True)  33.8 us
    pallas_call x1, Pallas kernels, local(): pl.pallas_call(fold_kernel, out_shape=jax.ShapeDtypeStruct((slots, 2, val...  3.97 us

profile of v19, /device:TPU:1, one launch (start us, length us, event | category | flops | bytes accessed | tf_op | source)
XLA Modules:
  0.0 38.8 jit_solution(11372941285238045800)
XLA Ops:
  0.0 4.0 %shard_map.73 = bf16[256,2,384]{2,1,0:T(2,128)(2,1)} custom-call(f32[2]{0:T(128)} %w_ref.1, bf16[129]{0:T(256)(128)(2,1)} %taps_ref.1, bf16[16,128]{1,0:T(8,128)(2,1)} %bitcast.5, bf16[16,128]{1,0:T(8,128)(2,1)} %bitcast.6, bf16[2,3,128,1024]{3,2,1,0:T(8,128)(2,1)} %bitcast.4, s32[256]{0:T(256)} %bitcast.7, s32[256]{0:T(256)} %owner_ref.1), custom_call_target="tpu_custom_call" | custom-call | tf_op jit(solution)/shard_map/pallas_call | solution.py:89
  4.0 33.8 %all_to_all.5 = bf16[256,2,384]{2,1,0:T(2,128)(2,1)S(1)} all-to-all(bf16[256,2,384]{2,1,0:T(2,128)(2,1)} %shard_map.73), channel_id=1, replica_groups=mesh['grp'=8,'tile'=32] {'grp','tile'}, dimensions={0} | all-to-all | bytes 786432 | tf_op jit(solution)/shard_map/all_to_all | solution.py:108
  37.8 0.4 %convert_reduce_fusion = f32[2,384]{1,0:T(2,128)S(1)} fusion(bf16[256,2,384]{2,1,0:T(2,128)(2,1)S(1)} %all_to_all.5), kind=kLoop, calls=%fused_computation | loop fusion | flops 392448 | bytes 396288 | tf_op jit(solution)/shard_map/reduce_sum | solution.py:109
  38.2 0.6 %reduce_sum.12 = f32[1,3,256]{2,0,1:T(1,128)} reshape(f32[2,384]{1,0:T(2,128)S(1)} %convert_reduce_fusion) | data formatting | bytes 6144 | tf_op jit(solution)/shard_map/reduce_sum | solution.py:109

commit v20 on v19

--- a/solution.py
+++ b/solution.py
@@ -40,7 +40,6 @@
         [smoothed[ctrl:, tile * (2 - d) : tile * (3 - d)] for d in range(3)], axis=0
     )
     rows_hi = rows_matrix.astype(jnp.bfloat16)
-    rows_lo = (rows_matrix - rows_hi.astype(jnp.float32)).astype(jnp.bfloat16)
     nt = (((1,), (1,)), ((), ()))
     for k in range(comps):
         summed = (sens_ref[0, k].astype(jnp.float32) * w_ref[0]).astype(jnp.float32)
@@ -51,8 +50,7 @@
         cols_hi = by_cols.astype(jnp.bfloat16)
         cols_lo = (by_cols - cols_hi.astype(jnp.float32)).astype(jnp.bfloat16)
         z = jnp.dot(rows_hi, cols_hi, preferred_element_type=jnp.float32)
-        z = z + jnp.dot(rows_hi, cols_lo, preferred_element_type=jnp.float32)
-        z = (z + jnp.dot(rows_lo, cols_hi, preferred_element_type=jnp.float32)).astype(jnp.bfloat16)
+        z = (z + jnp.dot(rows_hi, cols_lo, preferred_element_type=jnp.float32)).astype(jnp.bfloat16)
         block = ctrl * ctrl
         parts_ref[:, block * k : block * (k + 1)] = pltpu.einshape(
             "(dp)(yq)->(dy)(pq)", z, d=3, p=ctrl, y=col_tiles, q=ctrl

time: 38.9 us -> 38.9 us (level)
  no operation moved by 1% of the time
where the time goes in v20:
time: 38.9 us; the launch traced here: 38.8 us
  blocking collectives  33.8 us (87%)
  Pallas kernels  3.94 us (10%)
  local copies, waits for them, and re-layouts  0.6 us (2%)
  other arithmetic  0.41 us (1%)
    all_to_all x1, blocking collectives, local(): incoming = lax.all_to_all(outgoing, ('grp', 'tile'), 0, 0, tiled=True)  33.8 us
    pallas_call x1, Pallas kernels, local(): pl.pallas_call(fold_kernel, out_shape=jax.ShapeDtypeStruct((slots, 2, val...  3.94 us

profile of v20, /device:TPU:1, one launch (start us, length us, event | category | flops | bytes accessed | tf_op | source)
XLA Modules:
  0.0 38.8 jit_solution(17288508269652084559)
XLA Ops:
  0.0 3.9 %shard_map.73 = bf16[256,2,384]{2,1,0:T(2,128)(2,1)} custom-call(f32[2]{0:T(128)} %w_ref.1, bf16[129]{0:T(256)(128)(2,1)} %taps_ref.1, bf16[16,128]{1,0:T(8,128)(2,1)} %bitcast.5, bf16[16,128]{1,0:T(8,128)(2,1)} %bitcast.6, bf16[2,3,128,1024]{3,2,1,0:T(8,128)(2,1)} %bitcast.4, s32[256]{0:T(256)} %bitcast.7, s32[256]{0:T(256)} %owner_ref.1), custom_call_target="tpu_custom_call" | custom-call | tf_op jit(solution)/shard_map/pallas_call | solution.py:87
  3.9 33.8 %all_to_all.5 = bf16[256,2,384]{2,1,0:T(2,128)(2,1)S(1)} all-to-all(bf16[256,2,384]{2,1,0:T(2,128)(2,1)} %shard_map.73), channel_id=1, replica_groups=mesh['grp'=8,'tile'=32] {'grp','tile'}, dimensions={0} | all-to-all | bytes 786432 | tf_op jit(solution)/shard_map/all_to_all | solution.py:106
  37.8 0.4 %convert_reduce_fusion = f32[2,384]{1,0:T(2,128)S(1)} fusion(bf16[256,2,384]{2,1,0:T(2,128)(2,1)S(1)} %all_to_all.5), kind=kLoop, calls=%fused_computation | loop fusion | flops 392448 | bytes 396288 | tf_op jit(solution)/shard_map/reduce_sum | solution.py:107
  38.2 0.6 %reduce_sum.12 = f32[1,3,256]{2,0,1:T(1,128)} reshape(f32[2,384]{1,0:T(2,128)S(1)} %convert_reduce_fusion) | data formatting | bytes 6144 | tf_op jit(solution)/shard_map/reduce_sum | solution.py:107
